TPU v7x, 512 devices: a whole 4x8x8 slice. The times are simulated.
512 devices in a mesh: band: 16 (over y, core), dom: 32 (over z, x).
Axes of the slice: x: 4, y: 8, z: 8, core: 2. Of those that a mesh axis runs over, the one named last changes fastest.
Arguments:
- orbitals: float32 [32, 2, 256, 8, 128], P('band', None, 'dom'), may hold values from -6 to 6
- ace_vectors: float32 [16, 2, 256, 8, 128], P(None, None, 'dom'), may hold values from -0.078125 to 0.078125
- local_potential: float32 [256, 8, 128], P('dom'), may hold values from -1 to 1
- field_strength: float32 [2], replicated, may hold values from -2 to 2
- run_projectors: float32 [1024, 4, 256], P('dom'), may hold values from -0.09375 to 0.09375
- run_atom: int32 [1024], P('dom'), may hold values from 0 to 127, as said below
- run_count: int32 [1024], P('dom'), may hold values from 1 to 256, as said below
- run_start: int32 [1024], P('dom'), may hold values from 0 to 7936, as said below
- kb_energy: float32 [128], P('dom'), may hold values from 0.1 to 1
Outputs:
- propagated: float32 [32, 2, 256, 8, 128], P('band', None, 'dom')
- forces: float32 [2, 3, 128], P(None, None, 'dom')
Inputs may be any that keep to these rules, and one draw needn't show every extreme that they name: `run_atom`: atom a is owned by index a // 4 of dom. The 32 runs of one dom index name atoms of any one owner at most 2 times, and exactly 2 times for some owner. `run_count`: every dom index has a run of 256 points. `run_start`: every dom index has a run that starts at cell 8192 - 256.
All inputs are finite; a program needn't handle non-finite values.
Results may differ from a plain program's by a relative error of at most 0.0003.
Values sent between devices are 32-bit elements; how exact they have to be, the bound alone decides.
No kernel may reach another device: no remote copies, remote signals or barrier semaphores. Data moves between devices by JAX's collectives and lax.ppermute only.
A program may use at most 64 MiB of HBM per device.

v0:
```python
import jax
import jax.numpy as jnp
from jax import lax
from jax.sharding import PartitionSpec as P

STEPS = 2
TAYLOR = 4


spacing = 0.5
time_step = 0.04
highest = lax.Precision.HIGHEST


def extended_2(block, sides, width):
    for axis, dim in sides:
        count = lax.axis_size(axis)
        forward = [(i, i + 1) for i in range(count - 1)]
        backward = [(target, source) for source, target in forward]
        low = lax.ppermute(
            lax.slice_in_dim(block, block.shape[dim] - width, None, axis=dim), axis, forward
        )
        high = lax.ppermute(lax.slice_in_dim(block, 0, width, axis=dim), axis, backward)
        block = jnp.concatenate([low, block, high], axis=dim)
    return block


def laplace(extended):
    middle = extended[:, :, 2:-2]
    along_z = 16.0 * (extended[:, :, 3:-1] + extended[:, :, 1:-3]) - (
        extended[:, :, 4:] + extended[:, :, :-4]
    )
    along_x = 16.0 * (jnp.roll(middle, 1, 3) + jnp.roll(middle, -1, 3)) - (
        jnp.roll(middle, 2, 3) + jnp.roll(middle, -2, 3)
    )
    along_y = 16.0 * (jnp.roll(middle, 1, 4) + jnp.roll(middle, -1, 4)) - (
        jnp.roll(middle, 2, 4) + jnp.roll(middle, -2, 4)
    )
    return (along_z + along_x + along_y - 90.0 * middle) / (12.0 * spacing * spacing)


def projections(ace_rows, term):
    vector_count = ace_rows.shape[0]
    orbital_count = term.shape[0]
    products = lax.dot_general(
        ace_rows.reshape(vector_count * 2, -1),
        term.reshape(orbital_count * 2, -1),
        (((1,), (1,)), ((), ())),
        precision=highest,
        preferred_element_type=jnp.float32,
    )
    products = products.reshape(vector_count, 2, orbital_count, 2)
    return jnp.stack(
        [products[:, 0, :, 0] + products[:, 1, :, 1], products[:, 0, :, 1] - products[:, 1, :, 0]]
    )


def ace_weights(ace_rows, term):
    return lax.psum(projections(ace_rows, term), "dom")


def fock_term(ace_rows, weights):
    vector_count = ace_rows.shape[0]
    orbital_count = weights.shape[2]
    real_part = weights[0]
    imag_part = weights[1]
    coefficients = jnp.stack(
        [jnp.stack([real_part, imag_part], axis=-1), jnp.stack([-imag_part, real_part], axis=-1)],
        axis=1,
    )
    applied = lax.dot_general(
        coefficients.reshape(vector_count * 2, orbital_count * 2),
        ace_rows.reshape(vector_count * 2, -1),
        (((0,), (0,)), ((), ())),
        precision=highest,
        preferred_element_type=jnp.float32,
    )
    return applied.reshape((orbital_count, 2) + ace_rows.shape[2:])


def next_term(applied, degree):
    factor = time_step / degree
    return jnp.stack([factor * applied[:, 1], -factor * applied[:, 0]], axis=1)


def taylor_rounds(current, potential, ace_vectors):
    accumulated = current
    term = current
    for degree in range(1, TAYLOR + 1):
        extended = extended_2(term, (("dom", 2),), 2)
        weights = ace_weights(ace_vectors, term)
        applied = -0.5 * laplace(extended) + potential * term - fock_term(ace_vectors, weights)
        term = next_term(applied, degree)
        accumulated = accumulated + term
    return accumulated


def atom_partials(current, run_projectors, run_atom, run_count, run_start, kb_energy):
    row_count = current.shape[0] * 2
    point_count = run_projectors.shape[2]
    atom_dev = kb_energy.shape[0]
    dom_count = lax.axis_size("dom")
    slot_count = run_atom.shape[0]
    flattened = current.reshape(row_count, -1)

    def cut_run(run_begin):
        return lax.dynamic_slice_in_dim(flattened, run_begin, point_count, 1)

    pieces = jax.vmap(cut_run)(run_start)
    in_run = jnp.arange(point_count, dtype=jnp.int32)[None, :] < run_count[:, None]
    masked = jnp.where(in_run[:, None, :], run_projectors, 0.0)
    partials = jnp.einsum("scp,srp->scr", masked, pieces, precision=highest)
    capacity = 2 * slot_count // dom_count
    owner = run_atom // atom_dev
    slot_ids = jnp.arange(slot_count, dtype=jnp.int32)
    same_owner = (owner[:, None] == owner[None, :]) & (slot_ids[None, :] < slot_ids[:, None])
    owner_rank = jnp.sum(same_owner.astype(jnp.int32), axis=1)
    slot_pos = owner * capacity + owner_rank
    placement = jnp.arange(dom_count * capacity, dtype=jnp.int32)[:, None] == slot_pos[None, :]
    outgoing = jnp.einsum("ks,scr->kcr", placement.astype(jnp.float32), partials, precision=highest)
    atom_slots = jnp.max(jnp.where(placement, (run_atom % atom_dev)[None, :], -1), axis=1)
    received, received_ids = (
        lax.all_to_all(outgoing, "dom", split_axis=0, concat_axis=0, tiled=True),
        lax.all_to_all(atom_slots, "dom", split_axis=0, concat_axis=0, tiled=True),
    )
    matches = (received_ids[None, :] == jnp.arange(atom_dev, dtype=jnp.int32)[:, None]).astype(
        jnp.float32
    )
    atom_totals = jnp.einsum("ak,kcr->acr", matches, received, precision=highest)
    return (
        2.0
        * kb_energy[None, :]
        * jnp.einsum("ar,acr->ca", atom_totals[:, 0], atom_totals[:, 1:], precision=highest)
    )


def shards(
    orbitals,
    ace_vectors,
    local_potential,
    field_strength,
    run_projectors,
    run_atom,
    run_count,
    run_start,
    kb_energy,
):
    plane_count = orbitals.shape[2]
    plane_total = plane_count * lax.axis_size("dom")
    first_plane = lax.axis_index("dom") * plane_count
    height = (
        2.0
        * ((first_plane + jnp.arange(plane_count, dtype=jnp.int32)).astype(jnp.float32) + 0.5)
        / plane_total
        - 1.0
    )
    current = orbitals
    results = []
    for step_index in range(STEPS):
        strength = field_strength[step_index]
        current = taylor_rounds(
            current, local_potential + strength * height[:, None, None], ace_vectors
        )
        partial_force = atom_partials(
            current, run_projectors, run_atom, run_count, run_start, kb_energy
        )
        partial_force = lax.psum(partial_force, "band")
        results.append(partial_force)
    forces = jnp.stack(results)
    return (current, forces)


def solution(mesh):
    in_specs = (
        P("band", None, "dom", None, None),
        P(None, None, "dom", None, None),
        P("dom", None, None),
        P(),
        P("dom", None, None),
        P("dom"),
        P("dom"),
        P("dom"),
        P("dom"),
    )
    out_specs = (P("band", None, "dom", None, None), P(None, None, "dom"))
    return jax.shard_map(shards, mesh=mesh, in_specs=in_specs, out_specs=out_specs, check_vma=False)
```

profile of v0, /device:TPU:1, one launch (start us, length us, event | category | flops | bytes accessed | tf_op | source)
XLA Modules:
  0.0 938.4 jit_solution(7851821572021941752)
XLA Ops:
  2.0 4.5 collective-permute-start.1
  7.2 1.3 collective-permute-start
  10.0 14.1 %all-to-all-start = ((s32[32,2,1]{1,2,0:T(1,128)}), s32[32,2,1]{1,2,0:T(1,128)}, u32[]{:S(2)}, u32[]{:S(2)}) async-start(s32[32,2,1]{1,2,0:T(1,128)} %bitcast.89), calls=%async_computation | async-start | bytes 32768 | tf_op jit(solution)/shard_map/all_to_all | solution.py:124
  24.2 5.0 convolution_bitcast_fusion
  29.2 60.4 %psum.70 = f32[2,16,2]{1,2,0:T(2,128)S(1)} all-reduce(f32[2,16,2]{1,2,0:T(2,128)S(1)} %pad_maximum_fusion.23), channel_id=1, replica_groups=mesh['band'=16,'dom'=32] {'dom'}, use_global_device_ids=true, to_apply=%region_0.0 | all-reduce | flops 64 | bytes 512 | tf_op jit(solution)/shard_map/psum | solution.py:59
  96.3 1.2 broadcast_multiply_fusion.1
  111.2 1.4 reduce.31
  115.1 2.7 convolution_subtract_fusion.7
  119.4 55.7 %psum.71 = f32[2,16,2]{1,2,0:T(2,128)S(1)} all-reduce(f32[2,16,2]{1,2,0:T(2,128)S(1)} %pad_maximum_fusion.26), channel_id=1, replica_groups=mesh['band'=16,'dom'=32] {'dom'}, use_global_device_ids=true, to_apply=%region_1.2 | all-reduce | flops 64 | bytes 512 | tf_op jit(solution)/shard_map/psum | solution.py:59
  180.3 1.5 collective-permute-start.2
  181.8 4.6 collective-permute-start.3
  188.8 2.0 convolution_subtract_fusion.6
  192.4 57.9 %psum.72 = f32[2,16,2]{1,2,0:T(2,128)S(1)} all-reduce(f32[2,16,2]{1,2,0:T(2,128)S(1)} %pad_maximum_fusion.29), channel_id=1, replica_groups=mesh['band'=16,'dom'=32] {'dom'}, use_global_device_ids=true, to_apply=%region_2.3 | all-reduce | flops 64 | bytes 512 | tf_op jit(solution)/shard_map/psum | solution.py:59
  256.1 1.3 collective-permute-start.4
  257.4 4.6 collective-permute-start.5
  263.7 2.8 convolution_subtract_fusion.5
  268.1 57.5 %psum.73 = f32[2,16,2]{1,2,0:T(2,128)S(1)} all-reduce(f32[2,16,2]{1,2,0:T(2,128)S(1)} %pad_maximum_fusion.32), channel_id=1, replica_groups=mesh['band'=16,'dom'=32] {'dom'}, use_global_device_ids=true, to_apply=%region_3.4 | all-reduce | flops 64 | bytes 512 | tf_op jit(solution)/shard_map/psum | solution.py:59
  327.5 1.1 fusion.42
  331.5 1.3 collective-permute-start.6
  332.8 4.8 collective-permute-start.7
  339.8 2.9 convolution_subtract_fusion.4
  344.7 57.5 %psum.74 = f32[2,16,2]{1,2,0:T(2,128)S(1)} all-reduce(f32[2,16,2]{1,2,0:T(2,128)S(1)} %pad_maximum_fusion.35), channel_id=1, replica_groups=mesh['band'=16,'dom'=32] {'dom'}, use_global_device_ids=true, to_apply=%region_4.5 | all-reduce | flops 64 | bytes 512 | tf_op jit(solution)/shard_map/psum | solution.py:59
  408.9 43.4 %while.2 = (s32[]{:T(128)}, f32[4,8192]{1,0:T(4,128)S(1)}, s32[32,2]{0,1:T(2,128)S(1)}, f32[32,4,256]{2,1,0:T(4,128)S(1)}, s32[]{:T(128)}) while((s32[]{:T(128)}, f32[4,8192]{1,0:T(4,128)S(1)}, s32[32,2]{0,1:T(2,128)S(1)}, f32[32,4,256]{2,1,0:T(4,128)S(1)}, s32[]{:T(128)}) %tuple.152), condition=%wide.while_cond, body=%wide.while_body.sunk | while | flops 2 | bytes 8297 | solution.py:107
  454.4 16.1 %all-to-all-start.1 = ((f32[64,4,4]{2,1,0:T(4,128)}), f32[64,4,4]{2,1,0:T(4,128)S(1)}, u32[]{:S(2)}, u32[]{:S(2)}) async-start(f32[64,4,4]{2,1,0:T(4,128)} %copy.269), calls=%async_computation.1 | async-start | bytes 262144 | tf_op jit(solution)/shard_map/all_to_all | solution.py:123
  471.4 3.9 collective-permute-start.9
  475.3 1.3 collective-permute-start.8
  476.6 3.2 all-to-all-done.1
  481.9 3.3 convolution_subtract_fusion.3
  486.8 58.0 %psum.75 = f32[2,16,2]{1,2,0:T(2,128)S(1)} all-reduce(f32[2,16,2]{1,2,0:T(2,128)S(1)} %pad_maximum_fusion.38), channel_id=1, replica_groups=mesh['band'=16,'dom'=32] {'dom'}, use_global_device_ids=true, to_apply=%region_5.6 | all-reduce | flops 64 | bytes 512 | tf_op jit(solution)/shard_map/psum | solution.py:59
  544.8 1.1 fusion.37
  545.9 1.1 fusion.38
  551.4 1.3 collective-permute-start.10
  552.7 5.0 collective-permute-start.11
  561.1 3.1 convolution_subtract_fusion.2
  565.8 56.2 %psum.76 = f32[2,16,2]{1,2,0:T(2,128)S(1)} all-reduce(f32[2,16,2]{1,2,0:T(2,128)S(1)} %pad_maximum_fusion.41), channel_id=1, replica_groups=mesh['band'=16,'dom'=32] {'dom'}, use_global_device_ids=true, to_apply=%region_6.7 | all-reduce | flops 64 | bytes 512 | tf_op jit(solution)/shard_map/psum | solution.py:59
  623.1 1.1 fusion.30
  624.5 1.1 fusion.26
  629.3 1.3 collective-permute-start.12
  630.6 4.6 collective-permute-start.13
  638.6 3.2 convolution_subtract_fusion.1
  643.3 56.6 %psum.77 = f32[2,16,2]{1,2,0:T(2,128)S(1)} all-reduce(f32[2,16,2]{1,2,0:T(2,128)S(1)} %pad_maximum_fusion.44), channel_id=1, replica_groups=mesh['band'=16,'dom'=32] {'dom'}, use_global_device_ids=true, to_apply=%region_7.8 | all-reduce | flops 64 | bytes 512 | tf_op jit(solution)/shard_map/psum | solution.py:59
  704.5 1.3 collective-permute-start.14
  705.8 4.7 collective-permute-start.15
  712.8 2.0 convolution_subtract_fusion
  716.6 39.1 %while.3 = (s32[]{:T(128)}, f32[4,8192]{1,0:T(4,128)S(1)}, s32[32,2]{0,1:T(2,128)S(1)}, f32[32,4,256]{2,1,0:T(4,128)S(1)}, s32[]{:T(128)}) while((s32[]{:T(128)}, f32[4,8192]{1,0:T(4,128)S(1)}, s32[32,2]{0,1:T(2,128)S(1)}, f32[32,4,256]{2,1,0:T(4,128)S(1)}, s32[]{:T(128)}) %tuple.158), condition=%wide.while_cond.1, body=%wide.while_body.1.sunk | while | flops 2 | bytes 8297 | solution.py:107
  757.8 20.5 %all-to-all-start.2 = ((f32[64,4,4]{2,1,0:T(4,128)}), f32[64,4,4]{2,1,0:T(4,128)S(1)}, u32[]{:S(2)}, u32[]{:S(2)}) async-start(f32[64,4,4]{2,1,0:T(4,128)} %copy.273), calls=%async_computation.2 | async-start | bytes 262144 | tf_op jit(solution)/shard_map/all_to_all | solution.py:123
  778.6 9.1 all-to-all-done.2
  788.7 149.0 %all-reduce.1 = (f32[1,3,4]{2,1,0:T(4,128)S(1)}, f32[1,3,4]{2,1,0:T(4,128)S(1)}) all-reduce(f32[1,3,4]{2,1,0:T(4,128)S(1)} %get-tuple-element.269, f32[1,3,4]{2,1,0:T(4,128)S(1)} %get-tuple-element.268), channel_id=1, replica_groups=mesh['band'=16,'dom'=32] {'band'}, use_global_device_ids=true, to_apply=%region_11.12 | all-reduce | flops 24 | bytes 192 | tf_op jit(solution)/shard_map/psum | solution.py:167
  (621 shorter events, 181.7 us)
Async XLA Ops:
  1.4 22.7 %copy-start = (f32[2,2,8,8,128]{4,3,2,1,0:T(8,128)S(1)}, f32[2,2,8,8,128]{4,3,2,1,0:T(8,128)}, u32[]{:S(2)}) copy-start(f32[2,2,8,8,128]{4,3,2,1,0:T(8,128)} %param.9) | copy-start | bytes 393220
  2.0 111.2 %collective-permute-start.1 = (f32[2,2,2,8,128]{4,1,3,2,0:T(2,128)}, f32[2,2,2,8,128]{4,1,3,2,0:T(2,128)}, u32[]{:S(2)}, u32[]{:S(2)}) collective-permute-start(f32[2,2,2,8,128]{4,1,3,2,0:T(2,128)} %copy.378), channel_id=1, source_target_pairs={{0,1},{1,2},{2,3},{3,4},{4,5},{5,6},{6,7},{7,8},{8,9},{9,10},{10,1... | collective-permute-start | bytes 98312 | tf_op jit(solution)/shard_map/ppermute | solution.py:20
  6.6 1.9 copy-start.71
  7.2 107.0 %collective-permute-start = (f32[2,2,2,8,128]{4,1,3,2,0:T(2,128)}, f32[2,2,2,8,128]{4,1,3,2,0:T(2,128)}, u32[]{:S(2)}, u32[]{:S(2)}) collective-permute-start(f32[2,2,2,8,128]{4,1,3,2,0:T(2,128)} %copy.379), channel_id=1, source_target_pairs={{1,0},{2,1},{3,2},{4,3},{5,4},{6,5},{7,6},{8,7},{9,8},{10,9},{11,1... | collective-permute-start | bytes 98312 | tf_op jit(solution)/shard_map/ppermute | solution.py:23
  10.0 100.7 %all-to-all-start = ((s32[32,2,1]{1,2,0:T(1,128)}), s32[32,2,1]{1,2,0:T(1,128)}, u32[]{:S(2)}, u32[]{:S(2)}) async-start(s32[32,2,1]{1,2,0:T(1,128)} %bitcast.89), calls=%async_computation | async-start | bytes 32768 | tf_op jit(solution)/shard_map/all_to_all | solution.py:124
  91.7 6.5 copy-start.1
  93.8 1.3 copy-start.72
  93.8 1.9 copy-start.68
  93.8 1.9 copy-start.73
  94.5 3.0 copy-start.44
  106.3 2.1 copy-start.11
  113.3 1.8 copy-start.52
  113.3 1.8 copy-start.53
  180.3 6.3 collective-permute-start.2
  181.8 5.3 collective-permute-start.3
  186.6 1.5 copy-start.28
  186.6 1.5 copy-start.29
  186.6 1.5 copy-start.38
  186.6 1.5 copy-start.39
  256.1 6.1 collective-permute-start.4
  257.4 5.3 collective-permute-start.5
  262.2 1.5 copy-start.20
  262.2 1.5 copy-start.30
  262.2 1.5 copy-start.31
  262.2 1.5 copy-start.40
  262.3 1.5 copy-start.41
  331.5 6.3 collective-permute-start.6
  332.8 5.3 collective-permute-start.7
  337.8 1.3 copy-start.15
  337.8 1.3 copy-start.21
  337.8 1.3 copy-start.22
  408.8 43.5 %copy-start.9 = (f32[32,4,256]{2,1,0:T(4,128)S(1)}, f32[32,4,256]{2,1,0:T(4,128)}, u32[]{:S(2)}) copy-start(f32[32,4,256]{2,1,0:T(4,128)} %param.13) | copy-start | bytes 393220
  454.4 25.4 %all-to-all-start.1 = ((f32[64,4,4]{2,1,0:T(4,128)}), f32[64,4,4]{2,1,0:T(4,128)S(1)}, u32[]{:S(2)}, u32[]{:S(2)}) async-start(f32[64,4,4]{2,1,0:T(4,128)} %copy.269), calls=%async_computation.1 | async-start | bytes 262144 | tf_op jit(solution)/shard_map/all_to_all | solution.py:123
  471.4 9.8 %copy-start.27 = (f32[2,2,8,8,126]{4,1,3,2,0:T(2,128)S(1)}, f32[2,2,8,8,126]{4,1,3,2,0:T(2,128)}, u32[]{:S(2)}) copy-start(f32[2,2,8,8,126]{4,1,3,2,0:T(2,128)} %get-tuple-element.142) | copy-start | bytes 387076
  471.4 9.8 %collective-permute-start.9 = (f32[2,2,2,8,128]{4,1,3,2,0:T(2,128)}, f32[2,2,2,8,128]{4,1,3,2,0:T(2,128)}, u32[]{:S(2)}, u32[]{:S(2)}) collective-permute-start(f32[2,2,2,8,128]{4,1,3,2,0:T(2,128)} %get-tuple-element.127), channel_id=1, source_target_pairs={{0,1},{1,2},{2,3},{3,4},{4,5},{5,6},{6,7},{7,8},{8,9},{9,10},{10,1... | collective-permute-start | bytes 98312 | tf_op jit(solution)/shard_map/ppermute | solution.py:20
  475.3 5.9 collective-permute-start.8
  551.4 7.9 collective-permute-start.10
  552.7 6.6 collective-permute-start.11
  629.3 7.5 collective-permute-start.12
  630.6 6.2 collective-permute-start.13
  704.5 6.3 collective-permute-start.14
  705.8 5.3 collective-permute-start.15
  710.7 1.3 copy-start.35
  710.8 1.3 copy-start.36
  757.8 20.5 %slice-start = ((f32[4,4,4]{2,0,1:T(4,128)}), f32[4,3,4]{2,0,1:T(4,128)S(1)}, s32[]{:S(2)}) async-start(f32[4,4,4]{2,0,1:T(4,128)} %copy-done.51), calls=%async_computation.3 | async-start | bytes 12288 | tf_op jit(solution)/shard_map/slice | solution.py:133
  757.8 20.5 %copy-start.66 = (f32[4,1,4]{2,0,1:T(4,128)S(1)}, f32[4,1,4]{2,0,1:T(4,128)}, u32[]{:S(2)}) copy-start(f32[4,1,4]{2,0,1:T(4,128)} %slice.1403) | copy-start | bytes 196
  757.8 29.9 %all-to-all-start.2 = ((f32[64,4,4]{2,1,0:T(4,128)}), f32[64,4,4]{2,1,0:T(4,128)S(1)}, u32[]{:S(2)}, u32[]{:S(2)}) async-start(f32[64,4,4]{2,1,0:T(4,128)} %copy.273), calls=%async_computation.2 | async-start | bytes 262144 | tf_op jit(solution)/shard_map/all_to_all | solution.py:123
  778.5 9.2 copy-start.65
  (49 other events, 43.5 us)
where the time goes:
time: 950 us; the launch traced here: 938 us
  blocking collectives  609 us (64%)
  local copies, waits for them, and re-layouts  129 us (14%)
  starting transfers between devices  97.9 us (10%)
  other arithmetic  50.1 us (5%)
  matrix products  36 us (4%)
  waiting for transfers between devices  13.9 us (1%)
    psum x8, blocking collectives, ace_weights(): return lax.psum(projections(ace_rows, term), 'dom')  460 us
    psum x1, blocking collectives, shards(): partial_force = lax.psum(partial_force, 'band')  149 us
    gather x192, local copies, waits for them, and re-layouts  82.4 us
    ppermute x8, starting transfers between devices, extended_2(): lax.ppermute(lax.slice_in_dim(block, block.shape[dim] - width, None, axis...  36.6 us
    all_to_all x2, starting transfers between devices, atom_partials(): lax.all_to_all(outgoing, 'dom', split_axis=0, concat_axis=0, tiled=True)  36.6 us
    another operation x60, other arithmetic, next_term(): return jnp.stack([factor * applied[:, 1], -factor * applied[:, 0]], axis=1)  35.7 us
    unnamed x177, local copies, waits for them, and re-layouts  22.7 us
    dot_general x8, matrix products, fock_term(): lax.dot_general(coefficients.reshape(vector_count * 2, orbital_count * 2)...  22.2 us
  transfers between devices with their start and end apart: 19, of which 6 were waited for; matrix products, arithmetic and copies ran while one was open for 3% of the time, Pallas kernels for 0%

commit v1 on v0

--- a/solution.py
+++ b/solution.py
@@ -55,8 +55,14 @@
     )
 
 
+def exchange_sum(x, axis):
+    count = lax.axis_size(axis)
+    copies = jnp.broadcast_to(x[None], (count,) + x.shape)
+    return jnp.sum(lax.all_to_all(copies, axis, 0, 0, tiled=False), axis=0)
+
+
 def ace_weights(ace_rows, term):
-    return lax.psum(projections(ace_rows, term), "dom")
+    return exchange_sum(projections(ace_rows, term), "dom")
 
 
 def fock_term(ace_rows, weights):

time: 950 us -> 471 us (0.50)
  blocking collectives: 609 us -> 41.9 us
  starting transfers between devices: 97.9 us -> 152 us
  waiting for transfers between devices: 13.9 us -> 40.6 us
    psum x8 -> x0, blocking collectives: 460 us -> none  [ace_weights(): return lax.psum(projections(ace_rows, term), 'dom')]
    psum x1, blocking collectives: 149 us -> 41.9 us  [shards(): partial_force = lax.psum(partial_force, 'band')]
    all_to_all x0 -> x8, starting transfers between devices: none -> 67.8 us  [exchange_sum(): return jnp.sum(lax.all_to_all(copies, axis, 0, 0, tiled=False), axis=0)]
    all_to_all x0 -> x8, waiting for transfers between devices: none -> 22.9 us  [exchange_sum(): return jnp.sum(lax.all_to_all(copies, axis, 0, 0, tiled=False), axis=0)]
    all_to_all x2, starting transfers between devices: 36.6 us -> 25.2 us  [atom_partials(): lax.all_to_all(outgoing, 'dom', split_axis=0, concat_axis=0, tiled=True)]
    unnamed x177 -> x193, local copies, waits for them, and re-layouts: 22.7 us -> 20.3 us
  transfers between devices with their start and end apart: 19 -> 27, of which waited for: 6 -> 9; matrix products, arithmetic and copies ran while one was open for 3% -> 16% of each run, Pallas kernels for 0% -> 0%
where the time goes in v1:
time: 471 us; the launch traced here: 464 us
  starting transfers between devices  152 us (32%)
  local copies, waits for them, and re-layouts  133 us (28%)
  other arithmetic  56.4 us (12%)
  blocking collectives  41.9 us (9%)
  waiting for transfers between devices  40.6 us (9%)
  matrix products  36.1 us (8%)
    gather x192, local copies, waits for them, and re-layouts  84.4 us
    all_to_all x8, starting transfers between devices, exchange_sum(): return jnp.sum(lax.all_to_all(copies, axis, 0, 0, tiled=False), axis=0)  67.8 us
    psum x1, blocking collectives, shards(): partial_force = lax.psum(partial_force, 'band')  41.9 us
    another operation x60, other arithmetic, next_term(): return jnp.stack([factor * applied[:, 1], -factor * applied[:, 0]], axis=1)  40.9 us
    ppermute x8, starting transfers between devices, extended_2(): lax.ppermute(lax.slice_in_dim(block, block.shape[dim] - width, None, axis...  35 us
    all_to_all x2, starting transfers between devices, atom_partials(): lax.all_to_all(outgoing, 'dom', split_axis=0, concat_axis=0, tiled=True)  25.2 us
    dot_general x8, matrix products, fock_term(): lax.dot_general(coefficients.reshape(vector_count * 2, orbital_count * 2)...  24.2 us
    all_to_all x8, waiting for transfers between devices, exchange_sum(): return jnp.sum(lax.all_to_all(copies, axis, 0, 0, tiled=False), axis=0)  22.9 us
  transfers between devices with their start and end apart: 27, of which 9 were waited for; matrix products, arithmetic and copies ran while one was open for 16% of the time, Pallas kernels for 0%

profile of v1, /device:TPU:1, one launch (start us, length us, event | category | flops | bytes accessed | tf_op | source)
XLA Modules:
  0.0 463.5 jit_solution(15513531178015909545)
XLA Ops:
  2.0 4.5 collective-permute-start.1
  7.2 1.3 collective-permute-start
  10.1 14.0 %all-to-all-start.8 = ((s32[32,2,1]{1,2,0:T(1,128)}), s32[32,2,1]{1,2,0:T(1,128)S(1)}, u32[]{:S(2)}, u32[]{:S(2)}) async-start(s32[32,2,1]{1,2,0:T(1,128)} %bitcast.89), calls=%async_computation.8 | async-start | bytes 32768 | tf_op jit(solution)/shard_map/all_to_all | solution.py:130
  29.0 3.8 convolution_bitcast_fusion
  36.1 9.6 %all-to-all-start = ((f32[32,2,16,2]{2,3,1,0:T(2,128)}), f32[32,2,16,2]{2,3,1,0:T(2,128)}, u32[]{:S(2)}, u32[]{:S(2)}) async-start(f32[32,2,16,2]{2,3,1,0:T(2,128)} %broadcast_in_dim.50), calls=%async_computation | async-start | bytes 131072 | tf_op jit(solution)/shard_map/all_to_all | solution.py:61
  63.5 2.7 convolution_subtract_fusion.7
  73.6 9.3 %all-to-all-start.1 = ((f32[32,2,16,2]{2,3,1,0:T(2,128)}), f32[32,2,16,2]{2,3,1,0:T(2,128)S(1)}, u32[]{:S(2)}, u32[]{:S(2)}) async-start(f32[32,2,16,2]{2,3,1,0:T(2,128)} %broadcast_in_dim.51), calls=%async_computation.1 | async-start | bytes 131072 | tf_op jit(solution)/shard_map/all_to_all | solution.py:61
  83.6 1.3 collective-permute-start.2
  84.9 4.8 %collective-permute-start.3 = (f32[2,2,2,8,128]{4,1,3,2,0:T(2,128)}, f32[2,2,2,8,128]{4,1,3,2,0:T(2,128)}, u32[]{:S(2)}, u32[]{:S(2)}) collective-permute-start(f32[2,2,2,8,128]{4,1,3,2,0:T(2,128)} %get-tuple-element.193), channel_id=1, source_target_pairs={{0,1},{1,2},{2,3},{3,4},{4,5},{5,6},{6,7},{7,8},{8,9},{9,10},{10,1... | collective-permute-start | bytes 98312 | tf_op jit(solution)/shard_map/ppermute | solution.py:20
  89.7 2.2 all-to-all-done.1
  93.4 2.8 convolution_subtract_fusion.6
  103.6 10.6 %all-to-all-start.2 = ((f32[32,2,16,2]{2,3,1,0:T(2,128)}), f32[32,2,16,2]{2,3,1,0:T(2,128)S(1)}, u32[]{:S(2)}, u32[]{:S(2)}) async-start(f32[32,2,16,2]{2,3,1,0:T(2,128)} %broadcast_in_dim.52), calls=%async_computation.2 | async-start | bytes 131072 | tf_op jit(solution)/shard_map/all_to_all | solution.py:61
  114.9 1.3 collective-permute-start.4
  116.2 4.6 collective-permute-start.5
  120.8 2.3 all-to-all-done.2
  125.3 3.0 convolution_subtract_fusion.5
  136.4 11.1 %all-to-all-start.3 = ((f32[32,2,16,2]{2,3,1,0:T(2,128)}), f32[32,2,16,2]{2,3,1,0:T(2,128)S(1)}, u32[]{:S(2)}, u32[]{:S(2)}) async-start(f32[32,2,16,2]{2,3,1,0:T(2,128)} %broadcast_in_dim.53), calls=%async_computation.3 | async-start | bytes 131072 | tf_op jit(solution)/shard_map/all_to_all | solution.py:61
  147.6 1.3 collective-permute-start.6
  148.9 4.6 collective-permute-start.7
  153.5 2.9 all-to-all-done.3
  157.8 3.0 convolution_subtract_fusion.4
  169.4 2.7 collective-permute-start.9
  172.1 1.3 collective-permute-start.8
  173.4 39.3 %while.2 = (s32[]{:T(128)}, f32[4,8192]{1,0:T(4,128)S(1)}, s32[32,2]{0,1:T(2,128)S(1)}, f32[32,4,256]{2,1,0:T(4,128)S(1)}, s32[]{:T(128)}) while((s32[]{:T(128)}, f32[4,8192]{1,0:T(4,128)S(1)}, s32[32,2]{0,1:T(2,128)S(1)}, f32[32,4,256]{2,1,0:T(4,128)S(1)}, s32[]{:T(128)}) %tuple.152), condition=%wide.while_cond, body=%wide.while_body.sunk | while | flops 2 | bytes 8297 | solution.py:113
  214.9 14.7 %all-to-all-start.9 = ((f32[64,4,4]{2,1,0:T(4,128)}), f32[64,4,4]{2,1,0:T(4,128)S(1)}, u32[]{:S(2)}, u32[]{:S(2)}) async-start(f32[64,4,4]{2,1,0:T(4,128)} %copy.285), calls=%async_computation.9 | async-start | bytes 262144 | tf_op jit(solution)/shard_map/all_to_all | solution.py:129
  230.4 8.7 %all-to-all-done.9 = f32[64,4,4]{2,1,0:T(4,128)S(1)} async-done(((f32[64,4,4]{2,1,0:T(4,128)}), f32[64,4,4]{2,1,0:T(4,128)S(1)}, u32[]{:S(2)}, u32[]{:S(2)}) %all-to-all-start.9) | async-done | bytes 4128 | tf_op jit(solution)/shard_map/all_to_all | solution.py:129
  239.7 4.2 all-to-all-start.4
  244.6 8.1 %all-to-all-done.4 = f32[32,2,16,2]{2,3,1,0:T(2,128)S(1)} async-done(((f32[32,2,16,2]{2,3,1,0:T(2,128)}), f32[32,2,16,2]{2,3,1,0:T(2,128)S(1)}, u32[]{:S(2)}, u32[]{:S(2)}) %all-to-all-start.4) | async-done | bytes 8224 | tf_op jit(solution)/shard_map/all_to_all | solution.py:61
  253.7 3.3 convolution_subtract_fusion.3
  265.9 3.9 all-to-all-start.5
  270.4 1.3 collective-permute-start.10
  271.7 4.6 collective-permute-start.11
  276.2 2.3 all-to-all-done.5
  281.4 3.1 convolution_subtract_fusion.2
  294.0 9.5 %all-to-all-start.6 = ((f32[32,2,16,2]{2,3,1,0:T(2,128)}), f32[32,2,16,2]{2,3,1,0:T(2,128)S(1)}, u32[]{:S(2)}, u32[]{:S(2)}) async-start(f32[32,2,16,2]{2,3,1,0:T(2,128)} %broadcast_in_dim.56), calls=%async_computation.6 | async-start | bytes 131072 | tf_op jit(solution)/shard_map/all_to_all | solution.py:61
  304.2 1.3 collective-permute-start.12
  305.5 4.6 collective-permute-start.13
  310.1 2.3 all-to-all-done.6
  315.2 3.2 convolution_subtract_fusion.1
  328.0 9.5 %all-to-all-start.7 = ((f32[32,2,16,2]{2,3,1,0:T(2,128)}), f32[32,2,16,2]{2,3,1,0:T(2,128)S(1)}, u32[]{:S(2)}, u32[]{:S(2)}) async-start(f32[32,2,16,2]{2,3,1,0:T(2,128)} %broadcast_in_dim.57), calls=%async_computation.7 | async-start | bytes 131072 | tf_op jit(solution)/shard_map/all_to_all | solution.py:61
  337.6 1.4 collective-permute-start.14
  339.0 4.6 collective-permute-start.15
  343.6 2.7 all-to-all-done.7
  347.9 3.0 convolution_subtract_fusion
  352.6 45.2 %while.3 = (s32[]{:T(128)}, f32[4,8192]{1,0:T(4,128)S(1)}, s32[32,2]{0,1:T(2,128)S(1)}, f32[32,4,256]{2,1,0:T(4,128)S(1)}, s32[]{:T(128)}) while((s32[]{:T(128)}, f32[4,8192]{1,0:T(4,128)S(1)}, s32[32,2]{0,1:T(2,128)S(1)}, f32[32,4,256]{2,1,0:T(4,128)S(1)}, s32[]{:T(128)}) %tuple.158), condition=%wide.while_cond.1, body=%wide.while_body.1.sunk | while | flops 2 | bytes 8297 | solution.py:113
  400.0 10.4 %all-to-all-start.10 = ((f32[64,4,4]{2,1,0:T(4,128)}), f32[64,4,4]{2,1,0:T(4,128)S(1)}, u32[]{:S(2)}, u32[]{:S(2)}) async-start(f32[64,4,4]{2,1,0:T(4,128)} %copy.289), calls=%async_computation.10 | async-start | bytes 262144 | tf_op jit(solution)/shard_map/all_to_all | solution.py:129
  410.7 9.1 %all-to-all-done.10 = f32[64,4,4]{2,1,0:T(4,128)S(1)} async-done(((f32[64,4,4]{2,1,0:T(4,128)}), f32[64,4,4]{2,1,0:T(4,128)S(1)}, u32[]{:S(2)}, u32[]{:S(2)}) %all-to-all-start.10) | async-done | bytes 4128 | tf_op jit(solution)/shard_map/all_to_all | solution.py:129
  420.8 41.9 %all-reduce.1 = (f32[1,3,4]{2,1,0:T(4,128)S(1)}, f32[1,3,4]{2,1,0:T(4,128)S(1)}) all-reduce(f32[1,3,4]{2,1,0:T(4,128)S(1)} %get-tuple-element.269, f32[1,3,4]{2,1,0:T(4,128)S(1)} %get-tuple-element.268), channel_id=1, replica_groups=mesh['band'=16,'dom'=32] {'band'}, use_global_device_ids=true, to_apply=%region_11.12 | all-reduce | flops 24 | bytes 192 | tf_op jit(solution)/shard_map/psum | solution.py:173
  (661 shorter events, 197.7 us)
Async XLA Ops:
  1.4 22.7 %copy-start = (f32[2,2,8,8,128]{4,3,2,1,0:T(8,128)S(1)}, f32[2,2,8,8,128]{4,3,2,1,0:T(8,128)}, u32[]{:S(2)}) copy-start(f32[2,2,8,8,128]{4,3,2,1,0:T(8,128)} %param.9) | copy-start | bytes 393220
  2.0 59.6 %collective-permute-start.1 = (f32[2,2,2,8,128]{4,1,3,2,0:T(2,128)}, f32[2,2,2,8,128]{4,1,3,2,0:T(2,128)}, u32[]{:S(2)}, u32[]{:S(2)}) collective-permute-start(f32[2,2,2,8,128]{4,1,3,2,0:T(2,128)} %copy.394), channel_id=1, source_target_pairs={{0,1},{1,2},{2,3},{3,4},{4,5},{5,6},{6,7},{7,8},{8,9},{9,10},{10,1... | collective-permute-start | bytes 98312 | tf_op jit(solution)/shard_map/ppermute | solution.py:20
  7.2 55.4 %collective-permute-start = (f32[2,2,2,8,128]{4,1,3,2,0:T(2,128)}, f32[2,2,2,8,128]{4,1,3,2,0:T(2,128)}, u32[]{:S(2)}, u32[]{:S(2)}) collective-permute-start(f32[2,2,2,8,128]{4,1,3,2,0:T(2,128)} %copy.395), channel_id=1, source_target_pairs={{1,0},{2,1},{3,2},{4,3},{5,4},{6,5},{7,6},{8,7},{9,8},{10,9},{11,1... | collective-permute-start | bytes 98312 | tf_op jit(solution)/shard_map/ppermute | solution.py:23
  10.1 25.3 %all-to-all-start.8 = ((s32[32,2,1]{1,2,0:T(1,128)}), s32[32,2,1]{1,2,0:T(1,128)S(1)}, u32[]{:S(2)}, u32[]{:S(2)}) async-start(s32[32,2,1]{1,2,0:T(1,128)} %bitcast.89), calls=%async_computation.8 | async-start | bytes 32768 | tf_op jit(solution)/shard_map/all_to_all | solution.py:130
  25.6 3.4 copy-start.1
  29.0 3.8 copy-start.76
  29.0 4.4 copy-start.80
  29.0 4.4 copy-start.77
  36.1 9.7 %copy-start.81 = (f32[4]{0:T(128)S(1)}, f32[4]{0:T(128)}, u32[]{:S(2)}) copy-start(f32[4]{0:T(128)} %param.17) | copy-start | bytes 52
  36.1 24.4 %all-to-all-start = ((f32[32,2,16,2]{2,3,1,0:T(2,128)}), f32[32,2,16,2]{2,3,1,0:T(2,128)}, u32[]{:S(2)}, u32[]{:S(2)}) async-start(f32[32,2,16,2]{2,3,1,0:T(2,128)} %broadcast_in_dim.50), calls=%async_computation | async-start | bytes 131072 | tf_op jit(solution)/shard_map/all_to_all | solution.py:61
  73.6 18.3 %all-to-all-start.1 = ((f32[32,2,16,2]{2,3,1,0:T(2,128)}), f32[32,2,16,2]{2,3,1,0:T(2,128)S(1)}, u32[]{:S(2)}, u32[]{:S(2)}) async-start(f32[32,2,16,2]{2,3,1,0:T(2,128)} %broadcast_in_dim.51), calls=%async_computation.1 | async-start | bytes 131072 | tf_op jit(solution)/shard_map/all_to_all | solution.py:61
  83.6 8.6 %collective-permute-start.2 = (f32[2,2,2,8,128]{4,1,3,2,0:T(2,128)}, f32[2,2,2,8,128]{4,1,3,2,0:T(2,128)}, u32[]{:S(2)}, u32[]{:S(2)}) collective-permute-start(f32[2,2,2,8,128]{4,1,3,2,0:T(2,128)} %get-tuple-element.192), channel_id=1, source_target_pairs={{1,0},{2,1},{3,2},{4,3},{5,4},{6,5},{7,6},{8,7},{9,8},{10,9},{11,1... | collective-permute-start | bytes 98312 | tf_op jit(solution)/shard_map/ppermute | solution.py:23
  84.9 7.4 %collective-permute-start.3 = (f32[2,2,2,8,128]{4,1,3,2,0:T(2,128)}, f32[2,2,2,8,128]{4,1,3,2,0:T(2,128)}, u32[]{:S(2)}, u32[]{:S(2)}) collective-permute-start(f32[2,2,2,8,128]{4,1,3,2,0:T(2,128)} %get-tuple-element.193), channel_id=1, source_target_pairs={{0,1},{1,2},{2,3},{3,4},{4,5},{5,6},{6,7},{7,8},{8,9},{9,10},{10,1... | collective-permute-start | bytes 98312 | tf_op jit(solution)/shard_map/ppermute | solution.py:20
  103.6 19.5 %all-to-all-start.2 = ((f32[32,2,16,2]{2,3,1,0:T(2,128)}), f32[32,2,16,2]{2,3,1,0:T(2,128)S(1)}, u32[]{:S(2)}, u32[]{:S(2)}) async-start(f32[32,2,16,2]{2,3,1,0:T(2,128)} %broadcast_in_dim.52), calls=%async_computation.2 | async-start | bytes 131072 | tf_op jit(solution)/shard_map/all_to_all | solution.py:61
  114.9 8.5 %collective-permute-start.4 = (f32[2,2,2,8,128]{4,1,3,2,0:T(2,128)}, f32[2,2,2,8,128]{4,1,3,2,0:T(2,128)S(1)}, u32[]{:S(2)}, u32[]{:S(2)}) collective-permute-start(f32[2,2,2,8,128]{4,1,3,2,0:T(2,128)} %get-tuple-element.170), channel_id=1, source_target_pairs={{1,0},{2,1},{3,2},{4,3},{5,4},{6,5},{7,6},{8,7},{9,8},{10,9},{11,1... | collective-permute-start | bytes 98312 | tf_op jit(solution)/shard_map/ppermute | solution.py:23
  116.2 7.3 %collective-permute-start.5 = (f32[2,2,2,8,128]{4,1,3,2,0:T(2,128)}, f32[2,2,2,8,128]{4,1,3,2,0:T(2,128)}, u32[]{:S(2)}, u32[]{:S(2)}) collective-permute-start(f32[2,2,2,8,128]{4,1,3,2,0:T(2,128)} %get-tuple-element.171), channel_id=1, source_target_pairs={{0,1},{1,2},{2,3},{3,4},{4,5},{5,6},{6,7},{7,8},{8,9},{9,10},{10,1... | collective-permute-start | bytes 98312 | tf_op jit(solution)/shard_map/ppermute | solution.py:20
  136.4 20.0 %all-to-all-start.3 = ((f32[32,2,16,2]{2,3,1,0:T(2,128)}), f32[32,2,16,2]{2,3,1,0:T(2,128)S(1)}, u32[]{:S(2)}, u32[]{:S(2)}) async-start(f32[32,2,16,2]{2,3,1,0:T(2,128)} %broadcast_in_dim.53), calls=%async_computation.3 | async-start | bytes 131072 | tf_op jit(solution)/shard_map/all_to_all | solution.py:61
  147.6 9.1 %collective-permute-start.6 = (f32[2,2,2,8,128]{4,1,3,2,0:T(2,128)}, f32[2,2,2,8,128]{4,1,3,2,0:T(2,128)}, u32[]{:S(2)}, u32[]{:S(2)}) collective-permute-start(f32[2,2,2,8,128]{4,1,3,2,0:T(2,128)} %get-tuple-element.148), channel_id=1, source_target_pairs={{1,0},{2,1},{3,2},{4,3},{5,4},{6,5},{7,6},{8,7},{9,8},{10,9},{11,1... | collective-permute-start | bytes 98312 | tf_op jit(solution)/shard_map/ppermute | solution.py:23
  148.9 7.9 %collective-permute-start.7 = (f32[2,2,2,8,128]{4,1,3,2,0:T(2,128)}, f32[2,2,2,8,128]{4,1,3,2,0:T(2,128)}, u32[]{:S(2)}, u32[]{:S(2)}) collective-permute-start(f32[2,2,2,8,128]{4,1,3,2,0:T(2,128)} %get-tuple-element.149), channel_id=1, source_target_pairs={{0,1},{1,2},{2,3},{3,4},{4,5},{5,6},{6,7},{7,8},{8,9},{9,10},{10,1... | collective-permute-start | bytes 98312 | tf_op jit(solution)/shard_map/ppermute | solution.py:20
  169.4 83.7 %collective-permute-start.9 = (f32[2,2,2,8,128]{4,1,3,2,0:T(2,128)}, f32[2,2,2,8,128]{4,1,3,2,0:T(2,128)}, u32[]{:S(2)}, u32[]{:S(2)}) collective-permute-start(f32[2,2,2,8,128]{4,1,3,2,0:T(2,128)} %get-tuple-element.127), channel_id=1, source_target_pairs={{0,1},{1,2},{2,3},{3,4},{4,5},{5,6},{6,7},{7,8},{8,9},{9,10},{10,1... | collective-permute-start | bytes 98312 | tf_op jit(solution)/shard_map/ppermute | solution.py:20
  172.1 80.9 %collective-permute-start.8 = (f32[2,2,2,8,128]{4,1,3,2,0:T(2,128)}, f32[2,2,2,8,128]{4,1,3,2,0:T(2,128)}, u32[]{:S(2)}, u32[]{:S(2)}) collective-permute-start(f32[2,2,2,8,128]{4,1,3,2,0:T(2,128)} %get-tuple-element.126), channel_id=1, source_target_pairs={{1,0},{2,1},{3,2},{4,3},{5,4},{6,5},{7,6},{8,7},{9,8},{10,9},{11,1... | collective-permute-start | bytes 98312 | tf_op jit(solution)/shard_map/ppermute | solution.py:23
  173.4 39.4 %copy-start.9 = (f32[32,4,256]{2,1,0:T(4,128)S(1)}, f32[32,4,256]{2,1,0:T(4,128)}, u32[]{:S(2)}) copy-start(f32[32,4,256]{2,1,0:T(4,128)} %param.13) | copy-start | bytes 393220
  214.9 24.1 %all-to-all-start.9 = ((f32[64,4,4]{2,1,0:T(4,128)}), f32[64,4,4]{2,1,0:T(4,128)S(1)}, u32[]{:S(2)}, u32[]{:S(2)}) async-start(f32[64,4,4]{2,1,0:T(4,128)} %copy.285), calls=%async_computation.9 | async-start | bytes 262144 | tf_op jit(solution)/shard_map/all_to_all | solution.py:129
  239.7 4.2 copy-start.72
  239.7 13.0 %all-to-all-start.4 = ((f32[32,2,16,2]{2,3,1,0:T(2,128)}), f32[32,2,16,2]{2,3,1,0:T(2,128)S(1)}, u32[]{:S(2)}, u32[]{:S(2)}) async-start(f32[32,2,16,2]{2,3,1,0:T(2,128)} %broadcast_in_dim.54), calls=%async_computation.4 | async-start | bytes 131072 | tf_op jit(solution)/shard_map/all_to_all | solution.py:61
  244.6 8.4 %copy-start.52 = (f32[2,2,8,6,128]{4,1,3,2,0:T(2,128)S(1)}, f32[2,2,8,6,128]{4,1,3,2,0:T(2,128)}, u32[]{:S(2)}) copy-start(f32[2,2,8,6,128]{4,1,3,2,0:T(2,128)} %get-tuple-element.134) | copy-start | bytes 294916
  265.9 12.7 %all-to-all-start.5 = ((f32[32,2,16,2]{2,3,1,0:T(2,128)}), f32[32,2,16,2]{2,3,1,0:T(2,128)S(1)}, u32[]{:S(2)}, u32[]{:S(2)}) async-start(f32[32,2,16,2]{2,3,1,0:T(2,128)} %broadcast_in_dim.55), calls=%async_computation.5 | async-start | bytes 131072 | tf_op jit(solution)/shard_map/all_to_all | solution.py:61
  269.7 11.7 %copy-start.37 = (f32[2,2,8,8,127]{4,1,3,2,0:T(2,128)S(1)}, f32[2,2,8,8,127]{4,1,3,2,0:T(2,128)}, u32[]{:S(2)}) copy-start(f32[2,2,8,8,127]{4,1,3,2,0:T(2,128)} %get-tuple-element.119) | copy-start | bytes 390148
  270.4 10.0 %collective-permute-start.10 = (f32[2,2,2,8,128]{4,1,3,2,0:T(2,128)}, f32[2,2,2,8,128]{4,1,3,2,0:T(2,128)}, u32[]{:S(2)}, u32[]{:S(2)}) collective-permute-start(f32[2,2,2,8,128]{4,1,3,2,0:T(2,128)} %get-tuple-element.106), channel_id=1, source_target_pairs={{1,0},{2,1},{3,2},{4,3},{5,4},{6,5},{7,6},{8,7},{9,8},{10,9},{11,1... | collective-permute-start | bytes 98312 | tf_op jit(solution)/shard_map/ppermute | solution.py:23
  271.7 8.7 %collective-permute-start.11 = (f32[2,2,2,8,128]{4,1,3,2,0:T(2,128)}, f32[2,2,2,8,128]{4,1,3,2,0:T(2,128)}, u32[]{:S(2)}, u32[]{:S(2)}) collective-permute-start(f32[2,2,2,8,128]{4,1,3,2,0:T(2,128)} %get-tuple-element.107), channel_id=1, source_target_pairs={{0,1},{1,2},{2,3},{3,4},{4,5},{5,6},{6,7},{7,8},{8,9},{9,10},{10,1... | collective-permute-start | bytes 98312 | tf_op jit(solution)/shard_map/ppermute | solution.py:20
  278.7 2.7 copy-start.36
  294.0 18.3 %all-to-all-start.6 = ((f32[32,2,16,2]{2,3,1,0:T(2,128)}), f32[32,2,16,2]{2,3,1,0:T(2,128)S(1)}, u32[]{:S(2)}, u32[]{:S(2)}) async-start(f32[32,2,16,2]{2,3,1,0:T(2,128)} %broadcast_in_dim.56), calls=%async_computation.6 | async-start | bytes 131072 | tf_op jit(solution)/shard_map/all_to_all | solution.py:61
  303.5 11.6 %copy-start.38 = (f32[2,2,8,8,127]{4,1,3,2,0:T(2,128)S(1)}, f32[2,2,8,8,127]{4,1,3,2,0:T(2,128)}, u32[]{:S(2)}) copy-start(f32[2,2,8,8,127]{4,1,3,2,0:T(2,128)} %get-tuple-element.96) | copy-start | bytes 390148
  304.2 9.9 %collective-permute-start.12 = (f32[2,2,2,8,128]{4,1,3,2,0:T(2,128)}, f32[2,2,2,8,128]{4,1,3,2,0:T(2,128)}, u32[]{:S(2)}, u32[]{:S(2)}) collective-permute-start(f32[2,2,2,8,128]{4,1,3,2,0:T(2,128)} %get-tuple-element.84), channel_id=1, source_target_pairs={{1,0},{2,1},{3,2},{4,3},{5,4},{6,5},{7,6},{8,7},{9,8},{10,9},{11,1... | collective-permute-start | bytes 98312 | tf_op jit(solution)/shard_map/ppermute | solution.py:23
  305.5 8.6 %collective-permute-start.13 = (f32[2,2,2,8,128]{4,1,3,2,0:T(2,128)}, f32[2,2,2,8,128]{4,1,3,2,0:T(2,128)}, u32[]{:S(2)}, u32[]{:S(2)}) collective-permute-start(f32[2,2,2,8,128]{4,1,3,2,0:T(2,128)} %get-tuple-element.85), channel_id=1, source_target_pairs={{0,1},{1,2},{2,3},{3,4},{4,5},{5,6},{6,7},{7,8},{8,9},{9,10},{10,1... | collective-permute-start | bytes 98312 | tf_op jit(solution)/shard_map/ppermute | solution.py:20
  312.4 2.7 copy-start.35
  326.1 21.6 %copy-start.43 = (f32[2,2,8,7,128]{4,1,3,2,0:T(2,128)S(1)}, f32[2,2,8,7,128]{4,1,3,2,0:T(2,128)}, u32[]{:S(2)}) copy-start(f32[2,2,8,7,128]{4,1,3,2,0:T(2,128)} %get-tuple-element.67) | copy-start | bytes 344068
  327.2 20.6 %copy-start.42 = (f32[2,2,8,7,128]{4,1,3,2,0:T(2,128)S(1)}, f32[2,2,8,7,128]{4,1,3,2,0:T(2,128)}, u32[]{:S(2)}) copy-start(f32[2,2,8,7,128]{4,1,3,2,0:T(2,128)} %get-tuple-element.66) | copy-start | bytes 344068
  327.3 20.5 %copy-start.23 = (f32[2,2,8,8,127]{4,1,3,2,0:T(2,128)S(1)}, f32[2,2,8,8,127]{4,1,3,2,0:T(2,128)}, u32[]{:S(2)}) copy-start(f32[2,2,8,8,127]{4,1,3,2,0:T(2,128)} %get-tuple-element.75) | copy-start | bytes 390148
  328.0 19.8 %copy-start.22 = (f32[2,2,8,8,127]{4,1,3,2,0:T(2,128)S(1)}, f32[2,2,8,8,127]{4,1,3,2,0:T(2,128)}, u32[]{:S(2)}) copy-start(f32[2,2,8,8,127]{4,1,3,2,0:T(2,128)} %get-tuple-element.74) | copy-start | bytes 390148
  328.0 18.4 %all-to-all-start.7 = ((f32[32,2,16,2]{2,3,1,0:T(2,128)}), f32[32,2,16,2]{2,3,1,0:T(2,128)S(1)}, u32[]{:S(2)}, u32[]{:S(2)}) async-start(f32[32,2,16,2]{2,3,1,0:T(2,128)} %broadcast_in_dim.57), calls=%async_computation.7 | async-start | bytes 131072 | tf_op jit(solution)/shard_map/all_to_all | solution.py:61
  337.5 10.3 %copy-start.17 = (f32[2,2,8,8,1]{4,1,3,2,0:T(2,128)S(1)}, f32[2,2,8,8,1]{4,1,3,2,0:T(2,128)}, u32[]{:S(2)}) copy-start(f32[2,2,8,8,1]{4,1,3,2,0:T(2,128)} %get-tuple-element.73) | copy-start | bytes 3076
  337.6 9.1 %collective-permute-start.14 = (f32[2,2,2,8,128]{4,1,3,2,0:T(2,128)}, f32[2,2,2,8,128]{4,1,3,2,0:T(2,128)}, u32[]{:S(2)}, u32[]{:S(2)}) collective-permute-start(f32[2,2,2,8,128]{4,1,3,2,0:T(2,128)} %get-tuple-element.62), channel_id=1, source_target_pairs={{1,0},{2,1},{3,2},{4,3},{5,4},{6,5},{7,6},{8,7},{9,8},{10,9},{11,1... | collective-permute-start | bytes 98312 | tf_op jit(solution)/shard_map/ppermute | solution.py:23
  339.0 7.7 %collective-permute-start.15 = (f32[2,2,2,8,128]{4,1,3,2,0:T(2,128)}, f32[2,2,2,8,128]{4,1,3,2,0:T(2,128)}, u32[]{:S(2)}, u32[]{:S(2)}) collective-permute-start(f32[2,2,2,8,128]{4,1,3,2,0:T(2,128)} %get-tuple-element.63), channel_id=1, source_target_pairs={{0,1},{1,2},{2,3},{3,4},{4,5},{5,6},{6,7},{7,8},{8,9},{9,10},{10,1... | collective-permute-start | bytes 98312 | tf_op jit(solution)/shard_map/ppermute | solution.py:20
  400.0 10.4 %slice-start = ((f32[4,4,4]{2,0,1:T(4,128)}), f32[4,3,4]{2,0,1:T(4,128)S(1)}, s32[]{:S(2)}) async-start(f32[4,4,4]{2,0,1:T(4,128)} %copy-done.64), calls=%async_computation.11 | async-start | bytes 12288 | tf_op jit(solution)/shard_map/slice | solution.py:139
  400.0 10.5 %copy-start.75 = (f32[4,1,4]{2,0,1:T(4,128)S(1)}, f32[4,1,4]{2,0,1:T(4,128)}, u32[]{:S(2)}) copy-start(f32[4,1,4]{2,0,1:T(4,128)} %slice.1403) | copy-start | bytes 196
  400.0 19.8 %all-to-all-start.10 = ((f32[64,4,4]{2,1,0:T(4,128)}), f32[64,4,4]{2,1,0:T(4,128)S(1)}, u32[]{:S(2)}, u32[]{:S(2)}) async-start(f32[64,4,4]{2,1,0:T(4,128)} %copy.289), calls=%async_computation.10 | async-start | bytes 262144 | tf_op jit(solution)/shard_map/all_to_all | solution.py:129
  410.6 9.2 %copy-start.73 = (s32[64]{0:T(128)S(1)}, s32[64]{0:T(128)}, u32[]{:S(2)}) copy-start(s32[64]{0:T(128)} %eq.29) | copy-start | bytes 772
  (65 other events, 68.7 us)

commit v2 on v1

--- a/solution.py
+++ b/solution.py
@@ -101,21 +101,40 @@
     return accumulated
 
 
-def atom_partials(current, run_projectors, run_atom, run_count, run_start, kb_energy):
-    row_count = current.shape[0] * 2
-    point_count = run_projectors.shape[2]
+def projector_matrix(run_projectors, run_count, run_start, cell_count):
+    slot_count, comp_count, point_count = run_projectors.shape
+    lanes = 128
+    tiles_out = cell_count // lanes
+    span = point_count // lanes + 1
+    points = jnp.arange(point_count, dtype=jnp.int32)
+    masked = jnp.where(points[None, None, :] < run_count[:, None, None], run_projectors, 0.0)
+    window = jnp.pad(masked, ((0, 0), (0, 0), (0, span * lanes - point_count)))
+    shift = run_start % lanes
+    amount = 1
+    while amount < lanes:
+        moved = jnp.pad(window[:, :, : window.shape[2] - amount], ((0, 0), (0, 0), (amount, 0)))
+        window = jnp.where(((shift // amount) % 2 == 1)[:, None, None], moved, window)
+        amount *= 2
+    window = window.reshape(slot_count, comp_count, span, lanes)
+    first_tile = run_start // lanes
+    tile_ids = jnp.arange(tiles_out, dtype=jnp.int32)
+    full = jnp.zeros((slot_count, comp_count, tiles_out, lanes), jnp.float32)
+    for offset in range(span):
+        hit = (tile_ids[None, :] == (first_tile + offset)[:, None])[:, None, :, None]
+        full = full + jnp.where(hit, window[:, :, offset][:, :, None, :], 0.0)
+    return full.reshape(slot_count * comp_count, cell_count)
+
+
+def run_partials(current, matrix, slot_count):
+    flattened = current.reshape(current.shape[0] * 2, -1)
+    products = jnp.einsum("kn,rn->kr", matrix, flattened, precision=highest)
+    return products.reshape(slot_count, -1, flattened.shape[0])
+
+
+def atom_forces(partials, run_atom, kb_energy):
     atom_dev = kb_energy.shape[0]
     dom_count = lax.axis_size("dom")
     slot_count = run_atom.shape[0]
-    flattened = current.reshape(row_count, -1)
-
-    def cut_run(run_begin):
-        return lax.dynamic_slice_in_dim(flattened, run_begin, point_count, 1)
-
-    pieces = jax.vmap(cut_run)(run_start)
-    in_run = jnp.arange(point_count, dtype=jnp.int32)[None, :] < run_count[:, None]
-    masked = jnp.where(in_run[:, None, :], run_projectors, 0.0)
-    partials = jnp.einsum("scp,srp->scr", masked, pieces, precision=highest)
     capacity = 2 * slot_count // dom_count
     owner = run_atom // atom_dev
     slot_ids = jnp.arange(slot_count, dtype=jnp.int32)
@@ -123,7 +142,7 @@
     owner_rank = jnp.sum(same_owner.astype(jnp.int32), axis=1)
     slot_pos = owner * capacity + owner_rank
     placement = jnp.arange(dom_count * capacity, dtype=jnp.int32)[:, None] == slot_pos[None, :]
-    outgoing = jnp.einsum("ks,scr->kcr", placement.astype(jnp.float32), partials, precision=highest)
+    outgoing = jnp.einsum("ks,stcr->ktcr", placement.astype(jnp.float32), partials, precision=highest)
     atom_slots = jnp.max(jnp.where(placement, (run_atom % atom_dev)[None, :], -1), axis=1)
     received, received_ids = (
         lax.all_to_all(outgoing, "dom", split_axis=0, concat_axis=0, tiled=True),
@@ -132,11 +151,11 @@
     matches = (received_ids[None, :] == jnp.arange(atom_dev, dtype=jnp.int32)[:, None]).astype(
         jnp.float32
     )
-    atom_totals = jnp.einsum("ak,kcr->acr", matches, received, precision=highest)
+    atom_totals = jnp.einsum("ak,ktcr->atcr", matches, received, precision=highest)
     return (
         2.0
-        * kb_energy[None, :]
-        * jnp.einsum("ar,acr->ca", atom_totals[:, 0], atom_totals[:, 1:], precision=highest)
+        * kb_energy[None, None, :]
+        * jnp.einsum("atr,atcr->tca", atom_totals[:, :, 0], atom_totals[:, :, 1:], precision=highest)
     )
 
 
@@ -160,6 +179,9 @@
         / plane_total
         - 1.0
     )
+    slot_count = run_projectors.shape[0]
+    cell_count = orbitals[0, 0].size
+    matrix = projector_matrix(run_projectors, run_count, run_start, cell_count)
     current = orbitals
     results = []
     for step_index in range(STEPS):
@@ -167,12 +189,9 @@
         current = taylor_rounds(
             current, local_potential + strength * height[:, None, None], ace_vectors
         )
-        partial_force = atom_partials(
-            current, run_projectors, run_atom, run_count, run_start, kb_energy
-        )
-        partial_force = lax.psum(partial_force, "band")
-        results.append(partial_force)
-    forces = jnp.stack(results)
+        results.append(run_partials(current, matrix, slot_count))
+    partials = jnp.stack(results, axis=1)
+    forces = exchange_sum(atom_forces(partials, run_atom, kb_energy), "band")
     return (current, forces)
 
 

time: 471 us -> 367 us (0.78)
  local copies, waits for them, and re-layouts: 133 us -> 40.4 us
  matrix products: 36.1 us -> 58.2 us
  waiting for transfers between devices: 40.6 us -> 26.4 us
  blocking collectives: 41.9 us -> 29.7 us
    gather x192 -> x0, local copies, waits for them, and re-layouts: 84.4 us -> none
    psum x1 -> x0, blocking collectives: 41.9 us -> none  [shards(): partial_force = lax.psum(partial_force, 'band')]
    all_to_all x0 -> x1, blocking collectives: none -> 29.7 us  [exchange_sum(): return jnp.sum(lax.all_to_all(copies, axis, 0, 0, tiled=False), axis=0)]
    all_to_all x3 -> x2, starting transfers between devices: 39.2 us -> 16.8 us  [the longest x1 9.22 us: atom_forces(): lax.all_to_all(outgoing, 'dom', split_axis=0, concat_axis=0, tiled=True)]
    all_to_all x8, starting transfers between devices: 67.8 us -> 89.2 us  [exchange_sum(): return jnp.sum(lax.all_to_all(copies, axis, 0, 0, tiled=False), axis=0)]
    dot_general x6 -> x4, matrix products: 1.41 us -> 20.3 us  [the longest x2 19.9 us: run_partials(): products = jnp.einsum('kn,rn->kr', matrix, flattened, precision=highest)]
    unnamed x193 -> x68, local copies, waits for them, and re-layouts: 20.3 us -> 8.65 us
    all_to_all x3 -> x2, waiting for transfers between devices: 17.7 us -> 9.07 us  [the longest x1 9.07 us: atom_forces(): lax.all_to_all(outgoing, 'dom', split_axis=0, concat_axis=0, tiled=True)]
  transfers between devices with their start and end apart: 27 -> 26, of which waited for: 9 -> 7; matrix products, arithmetic and copies ran while one was open for 16% -> 18% of each run, Pallas kernels for 0% -> 0%
where the time goes in v2:
time: 367 us; the launch traced here: 362 us
  starting transfers between devices  148 us (40%)
  matrix products  58.2 us (16%)
  other arithmetic  55.9 us (15%)
  local copies, waits for them, and re-layouts  40.4 us (11%)
  blocking collectives  29.7 us (8%)
  waiting for transfers between devices  26.4 us (7%)
    all_to_all x8, starting transfers between devices, exchange_sum(): return jnp.sum(lax.all_to_all(copies, axis, 0, 0, tiled=False), axis=0)  89.2 us
    another operation x60, other arithmetic, next_term(): return jnp.stack([factor * applied[:, 1], -factor * applied[:, 0]], axis=1)  40.9 us
    ppermute x8, starting transfers between devices, extended_2(): lax.ppermute(lax.slice_in_dim(block, block.shape[dim] - width, None, axis...  32 us
    all_to_all x1, blocking collectives, exchange_sum(): return jnp.sum(lax.all_to_all(copies, axis, 0, 0, tiled=False), axis=0)  29.7 us
    dot_general x8, matrix products, fock_term(): lax.dot_general(coefficients.reshape(vector_count * 2, orbital_count * 2)...  26.3 us
    dot_general x2, matrix products, run_partials(): products = jnp.einsum('kn,rn->kr', matrix, flattened, precision=highest)  19.9 us
    all_to_all x8, waiting for transfers between devices, exchange_sum(): return jnp.sum(lax.all_to_all(copies, axis, 0, 0, tiled=False), axis=0)  17.3 us
    dot_general x8, matrix products, projections(): lax.dot_general(ace_rows.reshape(vector_count * 2, -1), term.reshape(orbi...  11.5 us
  transfers between devices with their start and end apart: 26, of which 7 were waited for; matrix products, arithmetic and copies ran while one was open for 18% of the time, Pallas kernels for 0%

profile of v2, /device:TPU:1, one launch (start us, length us, event | category | flops | bytes accessed | tf_op | source)
XLA Modules:
  0.0 361.9 jit_solution(8868417037368212688)
XLA Ops:
  0.7 5.1 %convolution_bitcast_fusion.2 = f32[16,2,2,2]{0,3,2,1:T(2,128)S(1)} fusion(f32[16,2,8,8,128,1]{4,3,2,1,0,5:T(8,128)} %bitcast.352, f32[2,2,8,8,128]{4,3,2,1,0:T(8,128)} %param.9), kind=kOutput, calls=%fused_computation.11 | convolution fusion | flops 12582912 | bytes 1180160 | tf_op jit(solution)/shard_map/dot_general | solution.py:45
  6.4 13.8 %all-to-all-start = ((f32[32,2,16,2]{2,3,1,0:T(2,128)}), f32[32,2,16,2]{2,3,1,0:T(2,128)}, u32[]{:S(2)}, u32[]{:S(2)}) async-start(f32[32,2,16,2]{2,3,1,0:T(2,128)} %broadcast_in_dim.202), calls=%async_computation | async-start | bytes 131072 | tf_op jit(solution)/shard_map/all_to_all | solution.py:61
  21.7 3.7 %collective-permute-start.1 = (f32[2,2,2,8,128]{4,1,3,2,0:T(2,128)}, f32[2,2,2,8,128]{4,1,3,2,0:T(2,128)}, u32[]{:S(2)}, u32[]{:S(2)}) collective-permute-start(f32[2,2,2,8,128]{4,1,3,2,0:T(2,128)} %copy.391), channel_id=1, source_target_pairs={{0,1},{1,2},{2,3},{3,4},{4,5},{5,6},{6,7},{7,8},{8,9},{9,10},{10,1... | collective-permute-start | bytes 98312 | tf_op jit(solution)/shard_map/ppermute | solution.py:20
  26.0 1.5 collective-permute-start
  31.8 1.6 fusion.263
  38.8 1.3 broadcast_multiply_fusion.1
  40.8 3.1 select_add_fusion
  51.2 5.0 %add.616 = f32[32,4,8192]{2,0,1:T(8,128)} reshape(f32[32,4,64,128]{3,2,0,1:T(8,128)} %select_add_fusion) | data formatting | bytes 8388608 | tf_op jit(solution)/shard_map/add | solution.py:124
  59.7 3.0 convolution_subtract_fusion.7
  70.2 10.4 %all-to-all-start.1 = ((f32[32,2,16,2]{2,3,1,0:T(2,128)}), f32[32,2,16,2]{2,3,1,0:T(2,128)S(1)}, u32[]{:S(2)}, u32[]{:S(2)}) async-start(f32[32,2,16,2]{2,3,1,0:T(2,128)} %broadcast_in_dim.203), calls=%async_computation.1 | async-start | bytes 131072 | tf_op jit(solution)/shard_map/all_to_all | solution.py:61
  81.2 1.3 collective-permute-start.2
  82.5 4.5 %collective-permute-start.3 = (f32[2,2,2,8,128]{4,1,3,2,0:T(2,128)}, f32[2,2,2,8,128]{4,1,3,2,0:T(2,128)S(1)}, u32[]{:S(2)}, u32[]{:S(2)}) collective-permute-start(f32[2,2,2,8,128]{4,1,3,2,0:T(2,128)} %get-tuple-element.166), channel_id=1, source_target_pairs={{0,1},{1,2},{2,3},{3,4},{4,5},{5,6},{6,7},{7,8},{8,9},{9,10},{10,1... | collective-permute-start | bytes 98312 | tf_op jit(solution)/shard_map/ppermute | solution.py:20
  87.0 2.4 all-to-all-done.1
  89.9 3.2 convolution_subtract_fusion.6
  100.6 10.8 %all-to-all-start.2 = ((f32[32,2,16,2]{2,3,1,0:T(2,128)}), f32[32,2,16,2]{2,3,1,0:T(2,128)S(1)}, u32[]{:S(2)}, u32[]{:S(2)}) async-start(f32[32,2,16,2]{2,3,1,0:T(2,128)} %broadcast_in_dim.204), calls=%async_computation.2 | async-start | bytes 131072 | tf_op jit(solution)/shard_map/all_to_all | solution.py:61
  112.0 1.3 collective-permute-start.4
  113.3 4.0 %collective-permute-start.5 = (f32[2,2,2,8,128]{4,1,3,2,0:T(2,128)}, f32[2,2,2,8,128]{4,1,3,2,0:T(2,128)S(1)}, u32[]{:S(2)}, u32[]{:S(2)}) collective-permute-start(f32[2,2,2,8,128]{4,1,3,2,0:T(2,128)} %get-tuple-element.144), channel_id=1, source_target_pairs={{0,1},{1,2},{2,3},{3,4},{4,5},{5,6},{6,7},{7,8},{8,9},{9,10},{10,1... | collective-permute-start | bytes 98312 | tf_op jit(solution)/shard_map/ppermute | solution.py:20
  117.3 2.9 all-to-all-done.2
  120.7 3.3 convolution_subtract_fusion.5
  132.0 10.8 %all-to-all-start.3 = ((f32[32,2,16,2]{2,3,1,0:T(2,128)}), f32[32,2,16,2]{2,3,1,0:T(2,128)S(1)}, u32[]{:S(2)}, u32[]{:S(2)}) async-start(f32[32,2,16,2]{2,3,1,0:T(2,128)} %broadcast_in_dim.205), calls=%async_computation.3 | async-start | bytes 131072 | tf_op jit(solution)/shard_map/all_to_all | solution.py:61
  143.5 1.3 collective-permute-start.6
  144.7 4.0 %collective-permute-start.7 = (f32[2,2,2,8,128]{4,1,3,2,0:T(2,128)}, f32[2,2,2,8,128]{4,1,3,2,0:T(2,128)S(1)}, u32[]{:S(2)}, u32[]{:S(2)}) collective-permute-start(f32[2,2,2,8,128]{4,1,3,2,0:T(2,128)} %get-tuple-element.122), channel_id=1, source_target_pairs={{0,1},{1,2},{2,3},{3,4},{4,5},{5,6},{6,7},{7,8},{8,9},{9,10},{10,1... | collective-permute-start | bytes 98312 | tf_op jit(solution)/shard_map/ppermute | solution.py:20
  148.7 2.9 all-to-all-done.3
  152.1 3.3 convolution_subtract_fusion.4
  163.6 10.8 %all-to-all-start.4 = ((f32[32,2,16,2]{2,3,1,0:T(2,128)}), f32[32,2,16,2]{2,3,1,0:T(2,128)S(1)}, u32[]{:S(2)}, u32[]{:S(2)}) async-start(f32[32,2,16,2]{2,3,1,0:T(2,128)} %broadcast_in_dim.206), calls=%async_computation.4 | async-start | bytes 131072 | tf_op jit(solution)/shard_map/all_to_all | solution.py:61
  174.4 3.8 %collective-permute-start.9 = (f32[2,2,2,8,128]{4,1,3,2,0:T(2,128)}, f32[2,2,2,8,128]{4,1,3,2,0:T(2,128)}, u32[]{:S(2)}, u32[]{:S(2)}) collective-permute-start(f32[2,2,2,8,128]{4,1,3,2,0:T(2,128)} %get-tuple-element.100), channel_id=1, source_target_pairs={{0,1},{1,2},{2,3},{3,4},{4,5},{5,6},{6,7},{7,8},{8,9},{9,10},{10,1... | collective-permute-start | bytes 98312 | tf_op jit(solution)/shard_map/ppermute | solution.py:20
  178.2 1.3 collective-permute-start.8
  179.5 9.9 %convolution_bitcast_fusion.1 = f32[32,1,4,4]{0,3,2,1:T(4,128)S(1)} fusion(f32[32,4,8192]{2,0,1:T(8,128)} %add.616, f32[4,8192,1]{1,0,2:T(4,128)S(1)} %reshape.755), kind=kOutput, calls=%fused_computation.10 | convolution fusion | flops 50331648 | bytes 4327424 | tf_op jit(solution)/shard_map/kn,rn->kr/dot_general | solution.py:130
  189.8 3.3 convolution_subtract_fusion.3
  201.9 10.4 %all-to-all-start.5 = ((f32[32,2,16,2]{2,3,1,0:T(2,128)}), f32[32,2,16,2]{2,3,1,0:T(2,128)S(1)}, u32[]{:S(2)}, u32[]{:S(2)}) async-start(f32[32,2,16,2]{2,3,1,0:T(2,128)} %broadcast_in_dim.207), calls=%async_computation.5 | async-start | bytes 131072 | tf_op jit(solution)/shard_map/all_to_all | solution.py:61
  213.0 1.3 collective-permute-start.10
  214.2 4.2 %collective-permute-start.11 = (f32[2,2,2,8,128]{4,1,3,2,0:T(2,128)}, f32[2,2,2,8,128]{4,1,3,2,0:T(2,128)S(1)}, u32[]{:S(2)}, u32[]{:S(2)}) collective-permute-start(f32[2,2,2,8,128]{4,1,3,2,0:T(2,128)} %get-tuple-element.80), channel_id=1, source_target_pairs={{0,1},{1,2},{2,3},{3,4},{4,5},{5,6},{6,7},{7,8},{8,9},{9,10},{10,1... | collective-permute-start | bytes 98312 | tf_op jit(solution)/shard_map/ppermute | solution.py:20
  218.4 2.7 all-to-all-done.5
  221.6 3.4 convolution_subtract_fusion.2
  233.9 11.1 %all-to-all-start.6 = ((f32[32,2,16,2]{2,3,1,0:T(2,128)}), f32[32,2,16,2]{2,3,1,0:T(2,128)S(1)}, u32[]{:S(2)}, u32[]{:S(2)}) async-start(f32[32,2,16,2]{2,3,1,0:T(2,128)} %broadcast_in_dim.208), calls=%async_computation.6 | async-start | bytes 131072 | tf_op jit(solution)/shard_map/all_to_all | solution.py:61
  247.0 4.0 %collective-permute-start.13 = (f32[2,2,2,8,128]{4,1,3,2,0:T(2,128)}, f32[2,2,2,8,128]{4,1,3,2,0:T(2,128)S(1)}, u32[]{:S(2)}, u32[]{:S(2)}) collective-permute-start(f32[2,2,2,8,128]{4,1,3,2,0:T(2,128)} %get-tuple-element.58), channel_id=1, source_target_pairs={{0,1},{1,2},{2,3},{3,4},{4,5},{5,6},{6,7},{7,8},{8,9},{9,10},{10,1... | collective-permute-start | bytes 98312 | tf_op jit(solution)/shard_map/ppermute | solution.py:20
  251.0 2.9 all-to-all-done.6
  254.4 3.4 convolution_subtract_fusion.1
  267.3 11.1 %all-to-all-start.7 = ((f32[32,2,16,2]{2,3,1,0:T(2,128)}), f32[32,2,16,2]{2,3,1,0:T(2,128)S(1)}, u32[]{:S(2)}, u32[]{:S(2)}) async-start(f32[32,2,16,2]{2,3,1,0:T(2,128)} %broadcast_in_dim.209), calls=%async_computation.7 | async-start | bytes 131072 | tf_op jit(solution)/shard_map/all_to_all | solution.py:61
  278.4 1.3 collective-permute-start.14
  279.7 4.0 %collective-permute-start.15 = (f32[2,2,2,8,128]{4,1,3,2,0:T(2,128)}, f32[2,2,2,8,128]{4,1,3,2,0:T(2,128)S(1)}, u32[]{:S(2)}, u32[]{:S(2)}) collective-permute-start(f32[2,2,2,8,128]{4,1,3,2,0:T(2,128)} %get-tuple-element.36), channel_id=1, source_target_pairs={{0,1},{1,2},{2,3},{3,4},{4,5},{5,6},{6,7},{7,8},{8,9},{9,10},{10,1... | collective-permute-start | bytes 98312 | tf_op jit(solution)/shard_map/ppermute | solution.py:20
  283.7 3.5 all-to-all-done.7
  287.2 7.6 %all-to-all-start.8 = ((s32[32,2,1]{1,2,0:T(1,128)}), s32[32,2,1]{1,2,0:T(1,128)S(1)}, u32[]{:S(2)}, u32[]{:S(2)}) async-start(s32[32,2,1]{1,2,0:T(1,128)} %bitcast.89), calls=%async_computation.8 | async-start | bytes 32768 | tf_op jit(solution)/shard_map/all_to_all | solution.py:149
  295.3 3.4 convolution_subtract_fusion
  299.9 9.9 %convolution_bitcast_fusion = f32[32,1,4,4]{0,3,2,1:T(4,128)S(1)} fusion(f32[32,4,8192]{2,0,1:T(8,128)} %add.616, f32[4,8192,1]{1,0,2:T(4,128)S(1)} %reshape.756), kind=kOutput, calls=%fused_computation.9 | convolution fusion | flops 50331648 | bytes 4327424 | tf_op jit(solution)/shard_map/kn,rn->kr/dot_general | solution.py:130
  311.0 9.2 %all-to-all-start.9 = ((f32[64,2,4,4]{3,2,1,0:T(4,128)}), f32[64,2,4,4]{3,2,1,0:T(4,128)S(1)}, u32[]{:S(2)}, u32[]{:S(2)}) async-start(f32[64,2,4,4]{3,2,1,0:T(4,128)} %copy.289), calls=%async_computation.9 | async-start | bytes 524288 | tf_op jit(solution)/shard_map/all_to_all | solution.py:148
  321.5 9.1 %all-to-all-done.9 = f32[64,2,4,4]{3,2,1,0:T(4,128)S(1)} async-done(((f32[64,2,4,4]{3,2,1,0:T(4,128)}), f32[64,2,4,4]{3,2,1,0:T(4,128)S(1)}, u32[]{:S(2)}, u32[]{:S(2)}) %all-to-all-start.9) | async-done | bytes 8224 | tf_op jit(solution)/shard_map/all_to_all | solution.py:148
  331.2 29.7 %all_to_all.59 = f32[16,2,3,4]{3,1,2,0:T(2,128)S(1)} all-to-all(f32[16,2,3,4]{3,1,2,0:T(2,128)S(1)} %broadcast_in_dim.231), channel_id=1, replica_groups=mesh['band'=16,'dom'=32] {'band'}, dimensions={0} | all-to-all | bytes 3072 | tf_op jit(solution)/shard_map/all_to_all | solution.py:61
  (350 shorter events, 93.7 us)
Async XLA Ops:
  0.6 33.8 %copy-start = (f32[2,2,8,8,128]{4,3,2,1,0:T(8,128)S(1)}, f32[2,2,8,8,128]{4,3,2,1,0:T(8,128)}, u32[]{:S(2)}) copy-start(f32[2,2,8,8,128]{4,3,2,1,0:T(8,128)} %param.9) | copy-start | bytes 393220
  0.6 35.2 %copy-start.18 = (s32[32]{0:T(128)S(1)}, s32[32]{0:T(128)}, u32[]{:S(2)}) copy-start(s32[32]{0:T(128)} %param.16) | copy-start | bytes 388
  0.7 35.2 %copy-start.15 = (f32[2]{0:T(128)S(1)}, f32[2]{0:T(128)}, u32[]{:S(2)}) copy-start(f32[2]{0:T(128)} %param.12) | copy-start | bytes 28
  0.7 35.8 %copy-start.16 = (s32[32]{0:T(128)S(1)}, s32[32]{0:T(128)}, u32[]{:S(2)}) copy-start(s32[32]{0:T(128)} %param.15) | copy-start | bytes 388
  0.7 35.8 %copy-start.5 = (f32[32,4,256]{2,1,0:T(4,128)S(1)}, f32[32,4,256]{2,1,0:T(4,128)}, u32[]{:S(2)}) copy-start(f32[32,4,256]{2,1,0:T(4,128)} %param.13) | copy-start | bytes 393220
  6.4 50.5 %all-to-all-start = ((f32[32,2,16,2]{2,3,1,0:T(2,128)}), f32[32,2,16,2]{2,3,1,0:T(2,128)}, u32[]{:S(2)}, u32[]{:S(2)}) async-start(f32[32,2,16,2]{2,3,1,0:T(2,128)} %broadcast_in_dim.202), calls=%async_computation | async-start | bytes 131072 | tf_op jit(solution)/shard_map/all_to_all | solution.py:61
  21.7 36.4 %collective-permute-start.1 = (f32[2,2,2,8,128]{4,1,3,2,0:T(2,128)}, f32[2,2,2,8,128]{4,1,3,2,0:T(2,128)}, u32[]{:S(2)}, u32[]{:S(2)}) collective-permute-start(f32[2,2,2,8,128]{4,1,3,2,0:T(2,128)} %copy.391), channel_id=1, source_target_pairs={{0,1},{1,2},{2,3},{3,4},{4,5},{5,6},{6,7},{7,8},{8,9},{9,10},{10,1... | collective-permute-start | bytes 98312 | tf_op jit(solution)/shard_map/ppermute | solution.py:20
  26.0 33.0 %collective-permute-start = (f32[2,2,2,8,128]{4,1,3,2,0:T(2,128)}, f32[2,2,2,8,128]{4,1,3,2,0:T(2,128)}, u32[]{:S(2)}, u32[]{:S(2)}) collective-permute-start(f32[2,2,2,8,128]{4,1,3,2,0:T(2,128)} %copy.392), channel_id=1, source_target_pairs={{1,0},{2,1},{3,2},{4,3},{5,4},{6,5},{7,6},{8,7},{9,8},{10,9},{11,1... | collective-permute-start | bytes 98312 | tf_op jit(solution)/shard_map/ppermute | solution.py:23
  29.6 8.9 %copy-start.19 = (s32[32]{0:T(128)S(1)}, s32[32]{0:T(128)}, u32[]{:S(2)}) copy-start(s32[32]{0:T(128)} %param.14) | copy-start | bytes 388
  29.6 10.5 %copy-start.11 = (f32[8,8,128]{2,1,0:T(8,128)S(1)}, f32[8,8,128]{2,1,0:T(8,128)}, u32[]{:S(2)}) copy-start(f32[8,8,128]{2,1,0:T(8,128)} %param.11) | copy-start | bytes 98308
  37.3 7.2 %copy-start.1 = (f32[16,2,8,8,128]{4,3,2,1,0:T(8,128)S(1)}, f32[16,2,8,8,128]{4,3,2,1,0:T(8,128)}, u32[]{:S(2)}) copy-start(f32[16,2,8,8,128]{4,3,2,1,0:T(8,128)} %param.10) | copy-start | bytes 3145732
  38.8 5.1 %copy-start.21 = (s32[32]{0:T(128)}, s32[32]{0:T(128)S(1)}, u32[]{:S(2)}) copy-start(s32[32]{0:T(128)S(1)} %multiply_add_fusion) | copy-start | bytes 388
  44.7 3.8 %copy-start.7 = (f32[2,2,8,2,128]{4,3,2,1,0:T(2,128)S(1)}, f32[2,2,8,2,128]{4,3,2,1,0:T(2,128)}, u32[]{:S(2)}) copy-start(f32[2,2,8,2,128]{4,3,2,1,0:T(2,128)} %get-tuple-element.193) | copy-start | bytes 98308
  44.7 4.4 %copy-start.10 = (f32[2,2,8,1,128]{4,3,2,1,0:T(1,128)S(1)}, f32[2,2,8,1,128]{4,3,2,1,0:T(1,128)}, u32[]{:S(2)}) copy-start(f32[2,2,8,1,128]{4,3,2,1,0:T(1,128)} %get-tuple-element.190) | copy-start | bytes 49156
  44.7 5.0 %copy-start.4 = (f32[2,2,8,7,128]{4,3,2,1,0:T(8,128)S(1)}, f32[2,2,8,7,128]{4,3,2,1,0:T(8,128)}, u32[]{:S(2)}) copy-start(f32[2,2,8,7,128]{4,3,2,1,0:T(8,128)} %get-tuple-element.192) | copy-start | bytes 344068
  44.7 5.1 %copy-start.3 = (f32[2,2,8,7,128]{4,3,2,1,0:T(8,128)S(1)}, f32[2,2,8,7,128]{4,3,2,1,0:T(8,128)}, u32[]{:S(2)}) copy-start(f32[2,2,8,7,128]{4,3,2,1,0:T(8,128)} %get-tuple-element.191) | copy-start | bytes 344068
  51.2 5.0 %copy-start.17 = (s32[64]{0:T(128)S(1)}, s32[64]{0:T(128)}, u32[]{:S(2)}) copy-start(s32[64]{0:T(128)} %select_reduce_fusion) | copy-start | bytes 772
  51.2 8.6 %copy-start.6 = (f32[2,2,8,8,2]{4,1,3,2,0:T(2,128)S(1)}, f32[2,2,8,8,2]{4,1,3,2,0:T(2,128)}, u32[]{:S(2)}) copy-start(f32[2,2,8,8,2]{4,1,3,2,0:T(2,128)} %copy.375) | copy-start | bytes 6148
  51.2 8.6 %copy-start.14 = (f32[2,2,8,1,128]{4,1,3,2,0:T(2,128)S(1)}, f32[2,2,8,1,128]{4,1,3,2,0:T(2,128)}, u32[]{:S(2)}) copy-start(f32[2,2,8,1,128]{4,1,3,2,0:T(2,128)} %copy.387) | copy-start | bytes 49156
  70.2 19.2 %all-to-all-start.1 = ((f32[32,2,16,2]{2,3,1,0:T(2,128)}), f32[32,2,16,2]{2,3,1,0:T(2,128)S(1)}, u32[]{:S(2)}, u32[]{:S(2)}) async-start(f32[32,2,16,2]{2,3,1,0:T(2,128)} %broadcast_in_dim.203), calls=%async_computation.1 | async-start | bytes 131072 | tf_op jit(solution)/shard_map/all_to_all | solution.py:61
  81.2 8.5 %collective-permute-start.2 = (f32[2,2,2,8,128]{4,1,3,2,0:T(2,128)}, f32[2,2,2,8,128]{4,1,3,2,0:T(2,128)S(1)}, u32[]{:S(2)}, u32[]{:S(2)}) collective-permute-start(f32[2,2,2,8,128]{4,1,3,2,0:T(2,128)} %get-tuple-element.165), channel_id=1, source_target_pairs={{1,0},{2,1},{3,2},{4,3},{5,4},{6,5},{7,6},{8,7},{9,8},{10,9},{11,1... | collective-permute-start | bytes 98312 | tf_op jit(solution)/shard_map/ppermute | solution.py:23
  82.5 7.2 %collective-permute-start.3 = (f32[2,2,2,8,128]{4,1,3,2,0:T(2,128)}, f32[2,2,2,8,128]{4,1,3,2,0:T(2,128)S(1)}, u32[]{:S(2)}, u32[]{:S(2)}) collective-permute-start(f32[2,2,2,8,128]{4,1,3,2,0:T(2,128)} %get-tuple-element.166), channel_id=1, source_target_pairs={{0,1},{1,2},{2,3},{3,4},{4,5},{5,6},{6,7},{7,8},{8,9},{9,10},{10,1... | collective-permute-start | bytes 98312 | tf_op jit(solution)/shard_map/ppermute | solution.py:20
  100.6 19.6 %all-to-all-start.2 = ((f32[32,2,16,2]{2,3,1,0:T(2,128)}), f32[32,2,16,2]{2,3,1,0:T(2,128)S(1)}, u32[]{:S(2)}, u32[]{:S(2)}) async-start(f32[32,2,16,2]{2,3,1,0:T(2,128)} %broadcast_in_dim.204), calls=%async_computation.2 | async-start | bytes 131072 | tf_op jit(solution)/shard_map/all_to_all | solution.py:61
  112.0 8.5 %collective-permute-start.4 = (f32[2,2,2,8,128]{4,1,3,2,0:T(2,128)}, f32[2,2,2,8,128]{4,1,3,2,0:T(2,128)S(1)}, u32[]{:S(2)}, u32[]{:S(2)}) collective-permute-start(f32[2,2,2,8,128]{4,1,3,2,0:T(2,128)} %get-tuple-element.143), channel_id=1, source_target_pairs={{1,0},{2,1},{3,2},{4,3},{5,4},{6,5},{7,6},{8,7},{9,8},{10,9},{11,1... | collective-permute-start | bytes 98312 | tf_op jit(solution)/shard_map/ppermute | solution.py:23
  113.3 7.2 %collective-permute-start.5 = (f32[2,2,2,8,128]{4,1,3,2,0:T(2,128)}, f32[2,2,2,8,128]{4,1,3,2,0:T(2,128)S(1)}, u32[]{:S(2)}, u32[]{:S(2)}) collective-permute-start(f32[2,2,2,8,128]{4,1,3,2,0:T(2,128)} %get-tuple-element.144), channel_id=1, source_target_pairs={{0,1},{1,2},{2,3},{3,4},{4,5},{5,6},{6,7},{7,8},{8,9},{9,10},{10,1... | collective-permute-start | bytes 98312 | tf_op jit(solution)/shard_map/ppermute | solution.py:20
  132.0 19.6 %all-to-all-start.3 = ((f32[32,2,16,2]{2,3,1,0:T(2,128)}), f32[32,2,16,2]{2,3,1,0:T(2,128)S(1)}, u32[]{:S(2)}, u32[]{:S(2)}) async-start(f32[32,2,16,2]{2,3,1,0:T(2,128)} %broadcast_in_dim.205), calls=%async_computation.3 | async-start | bytes 131072 | tf_op jit(solution)/shard_map/all_to_all | solution.py:61
  143.5 8.5 %collective-permute-start.6 = (f32[2,2,2,8,128]{4,1,3,2,0:T(2,128)}, f32[2,2,2,8,128]{4,1,3,2,0:T(2,128)S(1)}, u32[]{:S(2)}, u32[]{:S(2)}) collective-permute-start(f32[2,2,2,8,128]{4,1,3,2,0:T(2,128)} %get-tuple-element.121), channel_id=1, source_target_pairs={{1,0},{2,1},{3,2},{4,3},{5,4},{6,5},{7,6},{8,7},{9,8},{10,9},{11,1... | collective-permute-start | bytes 98312 | tf_op jit(solution)/shard_map/ppermute | solution.py:23
  144.7 7.2 %collective-permute-start.7 = (f32[2,2,2,8,128]{4,1,3,2,0:T(2,128)}, f32[2,2,2,8,128]{4,1,3,2,0:T(2,128)S(1)}, u32[]{:S(2)}, u32[]{:S(2)}) collective-permute-start(f32[2,2,2,8,128]{4,1,3,2,0:T(2,128)} %get-tuple-element.122), channel_id=1, source_target_pairs={{0,1},{1,2},{2,3},{3,4},{4,5},{5,6},{6,7},{7,8},{8,9},{9,10},{10,1... | collective-permute-start | bytes 98312 | tf_op jit(solution)/shard_map/ppermute | solution.py:20
  162.7 27.1 %copy-start.9 = (f32[2,2,8,8,126]{4,1,3,2,0:T(2,128)S(1)}, f32[2,2,8,8,126]{4,1,3,2,0:T(2,128)}, u32[]{:S(2)}) copy-start(f32[2,2,8,8,126]{4,1,3,2,0:T(2,128)} %get-tuple-element.115) | copy-start | bytes 387076
  162.7 27.1 %copy-start.12 = (f32[8,8,128]{2,1,0:T(8,128)S(1)}, f32[8,8,128]{2,1,0:T(8,128)}, u32[]{:S(2)}) copy-start(f32[8,8,128]{2,1,0:T(8,128)} %get-tuple-element.205) | copy-start | bytes 98308
  162.7 27.1 %copy-start.13 = (f32[2,2,8,2,128]{4,1,3,2,0:T(2,128)S(1)}, f32[2,2,8,2,128]{4,1,3,2,0:T(2,128)}, u32[]{:S(2)}) copy-start(f32[2,2,8,2,128]{4,1,3,2,0:T(2,128)} %get-tuple-element.105) | copy-start | bytes 98308
  163.6 25.8 %all-to-all-start.4 = ((f32[32,2,16,2]{2,3,1,0:T(2,128)}), f32[32,2,16,2]{2,3,1,0:T(2,128)S(1)}, u32[]{:S(2)}, u32[]{:S(2)}) async-start(f32[32,2,16,2]{2,3,1,0:T(2,128)} %broadcast_in_dim.206), calls=%async_computation.4 | async-start | bytes 131072 | tf_op jit(solution)/shard_map/all_to_all | solution.py:61
  174.4 15.3 %collective-permute-start.9 = (f32[2,2,2,8,128]{4,1,3,2,0:T(2,128)}, f32[2,2,2,8,128]{4,1,3,2,0:T(2,128)}, u32[]{:S(2)}, u32[]{:S(2)}) collective-permute-start(f32[2,2,2,8,128]{4,1,3,2,0:T(2,128)} %get-tuple-element.100), channel_id=1, source_target_pairs={{0,1},{1,2},{2,3},{3,4},{4,5},{5,6},{6,7},{7,8},{8,9},{9,10},{10,1... | collective-permute-start | bytes 98312 | tf_op jit(solution)/shard_map/ppermute | solution.py:20
  178.2 11.6 %collective-permute-start.8 = (f32[2,2,2,8,128]{4,1,3,2,0:T(2,128)}, f32[2,2,2,8,128]{4,1,3,2,0:T(2,128)}, u32[]{:S(2)}, u32[]{:S(2)}) collective-permute-start(f32[2,2,2,8,128]{4,1,3,2,0:T(2,128)} %get-tuple-element.99), channel_id=1, source_target_pairs={{1,0},{2,1},{3,2},{4,3},{5,4},{6,5},{7,6},{8,7},{9,8},{10,9},{11,1... | collective-permute-start | bytes 98312 | tf_op jit(solution)/shard_map/ppermute | solution.py:23
  201.9 19.2 %all-to-all-start.5 = ((f32[32,2,16,2]{2,3,1,0:T(2,128)}), f32[32,2,16,2]{2,3,1,0:T(2,128)S(1)}, u32[]{:S(2)}, u32[]{:S(2)}) async-start(f32[32,2,16,2]{2,3,1,0:T(2,128)} %broadcast_in_dim.207), calls=%async_computation.5 | async-start | bytes 131072 | tf_op jit(solution)/shard_map/all_to_all | solution.py:61
  213.0 8.5 %collective-permute-start.10 = (f32[2,2,2,8,128]{4,1,3,2,0:T(2,128)}, f32[2,2,2,8,128]{4,1,3,2,0:T(2,128)S(1)}, u32[]{:S(2)}, u32[]{:S(2)}) collective-permute-start(f32[2,2,2,8,128]{4,1,3,2,0:T(2,128)} %get-tuple-element.79), channel_id=1, source_target_pairs={{1,0},{2,1},{3,2},{4,3},{5,4},{6,5},{7,6},{8,7},{9,8},{10,9},{11,1... | collective-permute-start | bytes 98312 | tf_op jit(solution)/shard_map/ppermute | solution.py:23
  214.2 7.2 %collective-permute-start.11 = (f32[2,2,2,8,128]{4,1,3,2,0:T(2,128)}, f32[2,2,2,8,128]{4,1,3,2,0:T(2,128)S(1)}, u32[]{:S(2)}, u32[]{:S(2)}) collective-permute-start(f32[2,2,2,8,128]{4,1,3,2,0:T(2,128)} %get-tuple-element.80), channel_id=1, source_target_pairs={{0,1},{1,2},{2,3},{3,4},{4,5},{5,6},{6,7},{7,8},{8,9},{9,10},{10,1... | collective-permute-start | bytes 98312 | tf_op jit(solution)/shard_map/ppermute | solution.py:20
  233.9 20.0 %all-to-all-start.6 = ((f32[32,2,16,2]{2,3,1,0:T(2,128)}), f32[32,2,16,2]{2,3,1,0:T(2,128)S(1)}, u32[]{:S(2)}, u32[]{:S(2)}) async-start(f32[32,2,16,2]{2,3,1,0:T(2,128)} %broadcast_in_dim.208), calls=%async_computation.6 | async-start | bytes 131072 | tf_op jit(solution)/shard_map/all_to_all | solution.py:61
  245.7 8.5 %collective-permute-start.12 = (f32[2,2,2,8,128]{4,1,3,2,0:T(2,128)}, f32[2,2,2,8,128]{4,1,3,2,0:T(2,128)S(1)}, u32[]{:S(2)}, u32[]{:S(2)}) collective-permute-start(f32[2,2,2,8,128]{4,1,3,2,0:T(2,128)} %get-tuple-element.57), channel_id=1, source_target_pairs={{1,0},{2,1},{3,2},{4,3},{5,4},{6,5},{7,6},{8,7},{9,8},{10,9},{11,1... | collective-permute-start | bytes 98312 | tf_op jit(solution)/shard_map/ppermute | solution.py:23
  247.0 7.2 %collective-permute-start.13 = (f32[2,2,2,8,128]{4,1,3,2,0:T(2,128)}, f32[2,2,2,8,128]{4,1,3,2,0:T(2,128)S(1)}, u32[]{:S(2)}, u32[]{:S(2)}) collective-permute-start(f32[2,2,2,8,128]{4,1,3,2,0:T(2,128)} %get-tuple-element.58), channel_id=1, source_target_pairs={{0,1},{1,2},{2,3},{3,4},{4,5},{5,6},{6,7},{7,8},{8,9},{9,10},{10,1... | collective-permute-start | bytes 98312 | tf_op jit(solution)/shard_map/ppermute | solution.py:20
  267.3 19.9 %all-to-all-start.7 = ((f32[32,2,16,2]{2,3,1,0:T(2,128)}), f32[32,2,16,2]{2,3,1,0:T(2,128)S(1)}, u32[]{:S(2)}, u32[]{:S(2)}) async-start(f32[32,2,16,2]{2,3,1,0:T(2,128)} %broadcast_in_dim.209), calls=%async_computation.7 | async-start | bytes 131072 | tf_op jit(solution)/shard_map/all_to_all | solution.py:61
  278.4 16.7 %collective-permute-start.14 = (f32[2,2,2,8,128]{4,1,3,2,0:T(2,128)}, f32[2,2,2,8,128]{4,1,3,2,0:T(2,128)S(1)}, u32[]{:S(2)}, u32[]{:S(2)}) collective-permute-start(f32[2,2,2,8,128]{4,1,3,2,0:T(2,128)} %get-tuple-element.35), channel_id=1, source_target_pairs={{1,0},{2,1},{3,2},{4,3},{5,4},{6,5},{7,6},{8,7},{9,8},{10,9},{11,1... | collective-permute-start | bytes 98312 | tf_op jit(solution)/shard_map/ppermute | solution.py:23
  279.7 15.4 %collective-permute-start.15 = (f32[2,2,2,8,128]{4,1,3,2,0:T(2,128)}, f32[2,2,2,8,128]{4,1,3,2,0:T(2,128)S(1)}, u32[]{:S(2)}, u32[]{:S(2)}) collective-permute-start(f32[2,2,2,8,128]{4,1,3,2,0:T(2,128)} %get-tuple-element.36), channel_id=1, source_target_pairs={{0,1},{1,2},{2,3},{3,4},{4,5},{5,6},{6,7},{7,8},{8,9},{9,10},{10,1... | collective-permute-start | bytes 98312 | tf_op jit(solution)/shard_map/ppermute | solution.py:20
  287.2 23.8 %all-to-all-start.8 = ((s32[32,2,1]{1,2,0:T(1,128)}), s32[32,2,1]{1,2,0:T(1,128)S(1)}, u32[]{:S(2)}, u32[]{:S(2)}) async-start(s32[32,2,1]{1,2,0:T(1,128)} %bitcast.89), calls=%async_computation.8 | async-start | bytes 32768 | tf_op jit(solution)/shard_map/all_to_all | solution.py:149
  298.8 11.1 %copy-start.22 = (s32[32]{0:T(128)S(1)}, s32[32]{0:T(128)}, u32[]{:S(2)}) copy-start(s32[32]{0:T(128)} %copy-done.21) | copy-start | bytes 388
  298.8 21.4 %copy-start.20 = (f32[4]{0:T(128)S(1)}, f32[4]{0:T(128)}, u32[]{:S(2)}) copy-start(f32[4]{0:T(128)} %param.17) | copy-start | bytes 52
  299.9 61.6 %copy-start.2 = (f32[2,2,8,8,128]{4,3,2,1,0:T(8,128)}, f32[2,2,8,8,128]{4,3,2,1,0:T(8,128)S(1)}, u32[]{:S(2)}) copy-start(f32[2,2,8,8,128]{4,3,2,1,0:T(8,128)S(1)} %copy.292) | copy-start | bytes 393220
  311.0 19.6 %all-to-all-start.9 = ((f32[64,2,4,4]{3,2,1,0:T(4,128)}), f32[64,2,4,4]{3,2,1,0:T(4,128)S(1)}, u32[]{:S(2)}, u32[]{:S(2)}) async-start(f32[64,2,4,4]{3,2,1,0:T(4,128)} %copy.289), calls=%async_computation.9 | async-start | bytes 524288 | tf_op jit(solution)/shard_map/all_to_all | solution.py:148
  (1 other events, 1.8 us)
